TPU v7x, 32 devices: a whole 2x2x4 slice. The times are simulated.
32 devices in a mesh: section: 4 (over y, x), expert: 8 (over z, core).
Axes of the slice: x: 2, y: 2, z: 4, core: 2. Of those that a mesh axis runs over, the one named last changes fastest.
Arguments:
- layer_inputs: bfloat16 [4, 16, 64, 4096], P('section', None, 'expert'), may hold values from -6 to 6
- expert_ids: int32 [4, 16, 64, 2], P('section', None, 'expert'), may hold values from 0 to 7, all different within a row; in each aligned block of 8 rows (0 to 7, 8 to 15, ..., all dimensions but the last counted through in order) at most 3 rows name the same one
- gates: bfloat16 [4, 16, 64, 2], P('section', None, 'expert'), may hold values from 0.099609375 to 0.59765625
- w_gate: bfloat16 [4, 4096, 4096], P('section', None, 'expert'), may hold values from -0.09375 to 0.09375
- w_up: bfloat16 [4, 4096, 4096], P('section', None, 'expert'), may hold values from -0.09375 to 0.09375
- w_down: bfloat16 [4, 4096, 4096], P('section', 'expert'), may hold values from -0.25 to 0.25
- out_grad: bfloat16 [16, 64, 4096], P(None, 'expert'), may hold values from -6 to 6
Outputs:
- section_grads: bfloat16 [4, 16, 64, 4096], P('section', None, 'expert')
Inputs may be any that keep to these rules, and one draw needn't show every extreme that they name: `expert_ids`: within one micro-batch of one section, the 8 tokens of one expert index name each expert at most 3 times, and in some such groups one expert exactly 3 times; a token's 2 experts differ.
All inputs are finite; a program needn't handle non-finite values.
Results may differ from a plain program's by a relative error of at most 0.035.
Values may be sent and summed in bfloat16 or wider, within the bound.
No kernel may reach another device: no remote copies, remote signals or barrier semaphores. Data moves between devices by JAX's collectives and lax.ppermute only.
A program may use at most 64 MiB of HBM per device.

v0:
```python
import jax
import jax.numpy as jnp
from jax import lax
from jax.sharding import PartitionSpec as P

EXPERTS = 8
CAP = 3
CHUNK = 4


def passed_along(x, axis, by):
    length = lax.axis_size(axis)
    pairs = [(i, i + by) for i in range(length) if 0 <= i + by < length]
    return lax.ppermute(x, axis, pairs)


def selection(choices, capacity):
    token_count, top_count = (choices.shape[-2], choices.shape[-1])
    experts = jnp.arange(EXPERTS, dtype=jnp.int32)
    onehot = (choices[..., None] == experts).astype(jnp.int32)
    leading = onehot.shape[:-3]
    flattened = onehot.reshape(leading + (token_count * top_count, EXPERTS))
    before = jnp.cumsum(flattened, axis=-2) - flattened
    slot_index = jnp.sum((before * flattened).reshape(onehot.shape), axis=-1)
    places = jnp.arange(capacity, dtype=jnp.int32)
    in_slot = (slot_index[..., None] == places).astype(jnp.int32)
    return onehot[..., None] * in_slot[..., None, :]


def on_device(layer_inputs, expert_ids, gates, w_gate, w_up, w_down, out_grad):
    expert_count = lax.axis_size("expert")
    section_count = lax.axis_size("section")
    section_index = lax.axis_index("section")
    inputs = layer_inputs[0]
    gate_slice = w_gate[0]
    up_slice = w_up[0]
    down_t = w_down[0].T
    micro_count, token_count, model_width = inputs.shape
    hidden = gate_slice.shape[1]
    shards = expert_count // EXPERTS
    capacity = CAP
    slot_rows = expert_count * capacity
    chunk = CHUNK if micro_count % CHUNK == 0 else 1
    chunk_count = micro_count // chunk
    contract = (((1,), (1,)), ((), ()))
    selected = selection(expert_ids[0], capacity)
    dispatch = jnp.sum(selected, axis=2).astype(jnp.bfloat16)
    gate_values = gates[0].astype(jnp.float32)
    combine = jnp.sum(selected.astype(jnp.float32) * gate_values[..., None, None], axis=2).astype(
        jnp.bfloat16
    )

    def spread(rows):
        trailing = rows.shape[1:]
        rows = rows.astype(jnp.bfloat16)
        rows = jnp.broadcast_to(rows[:, None], (EXPERTS, shards) + trailing)
        return rows.reshape((expert_count,) + trailing)

    def backward_rows(grad_block, act, coef):
        down_grad = jnp.dot(grad_block, down_t, preferred_element_type=jnp.float32)
        dgate = (down_grad * coef).astype(jnp.bfloat16)
        dup = (down_grad * act).astype(jnp.bfloat16)
        total = lax.dot_general(dgate, gate_slice, contract, preferred_element_type=jnp.float32)
        total = total + lax.dot_general(dup, up_slice, contract, preferred_element_type=jnp.float32)
        return total.astype(jnp.bfloat16)

    def forward_chunk(first):
        inputs_chunk = lax.slice_in_dim(inputs, first, first + chunk, axis=0)
        dispatch_part = lax.slice_in_dim(dispatch, first, first + chunk, axis=0)
        outgoing = spread(
            jnp.einsum("mtec,mtd->ecmd", dispatch_part, inputs_chunk, preferred_element_type=jnp.float32)
        )
        received = lax.all_to_all(outgoing, "expert", split_axis=0, concat_axis=0, tiled=True)
        row_block = received.reshape(-1, model_width)
        pre_gate = jnp.dot(row_block, gate_slice, preferred_element_type=jnp.float32)
        pre_up = jnp.dot(row_block, up_slice, preferred_element_type=jnp.float32)
        sigmoid_gate = jax.nn.sigmoid(pre_gate)
        act = pre_gate * sigmoid_gate
        coef = pre_up * (sigmoid_gate * (1.0 + pre_gate * (1.0 - sigmoid_gate)))
        return act, coef

    def tick(tick_index, state_pair):
        incoming, results, act_all, coef_all = state_pair
        if tick_index < chunk_count:
            act_new, coef_new = forward_chunk(tick_index * chunk)
            act_all = act_all.at[tick_index].set(act_new)
            coef_all = coef_all.at[tick_index].set(coef_new)
        chunk_index = tick_index - (section_count - 1 - section_index)
        active = (chunk_index >= 0) & (chunk_index < chunk_count)
        start = jnp.clip(chunk_index, 0, chunk_count - 1) * chunk
        top_grad = lax.dynamic_slice_in_dim(out_grad, start, chunk, 0)
        grad_out = jnp.where(section_index == section_count - 1, top_grad, incoming)
        dispatch_chunk = lax.dynamic_slice_in_dim(dispatch, start, chunk, 0)
        combine_chunk = lax.dynamic_slice_in_dim(combine, start, chunk, 0)
        grad_rows = spread(
            jnp.einsum("mtec,mtd->ecmd", dispatch_chunk, grad_out, preferred_element_type=jnp.float32)
        )
        arrived = lax.all_to_all(grad_rows, "expert", split_axis=0, concat_axis=0, tiled=True)
        act_chunk = lax.dynamic_index_in_dim(act_all, start // chunk, 0, keepdims=False)
        coef_chunk = lax.dynamic_index_in_dim(coef_all, start // chunk, 0, keepdims=False)
        back = backward_rows(arrived.reshape(-1, model_width), act_chunk, coef_chunk)
        returned = lax.all_to_all(
            back.reshape(expert_count, capacity, chunk, model_width),
            "expert",
            split_axis=0,
            concat_axis=0,
            tiled=True,
        )
        returned = returned.reshape(EXPERTS, shards, capacity, chunk, model_width)
        mixed = jnp.einsum(
            "mtec,ekcmd->mtd", combine_chunk, returned, preferred_element_type=jnp.float32
        )
        grad_in = (grad_out.astype(jnp.float32) + mixed).astype(jnp.bfloat16)
        slot = (jnp.clip(chunk_index, -1, chunk_count) + 1) * chunk
        results = lax.dynamic_update_slice_in_dim(results, grad_in, slot, 0)
        passed = passed_along(grad_in, "section", -1)
        return (passed, results, act_all, coef_all)

    initial = (
        jnp.zeros((chunk, token_count, model_width), jnp.bfloat16),
        jnp.zeros((micro_count + 2 * chunk, token_count, model_width), jnp.bfloat16),
        jnp.zeros((chunk_count, expert_count * chunk * capacity, hidden), jnp.float32),
        jnp.zeros((chunk_count, expert_count * chunk * capacity, hidden), jnp.float32),
    )
    final_state = initial
    for tick_index in range(chunk_count + section_count - 1):
        final_state = tick(tick_index, final_state)
    return final_state[1][chunk : chunk + micro_count][None]


def solution(mesh):
    placed = (
        P("section", None, "expert", None),
        P("section", None, "expert", None),
        P("section", None, "expert", None),
        P("section", None, "expert"),
        P("section", None, "expert"),
        P("section", "expert", None),
        P(None, "expert", None),
    )
    return jax.shard_map(
        on_device,
        mesh=mesh,
        in_specs=placed,
        out_specs=P("section", None, "expert", None),
        check_vma=False,
    )
```

profile of v0, /device:TPU:0, one launch (start us, length us, event | category | flops | bytes accessed | tf_op | source)
XLA Modules:
  0.0 574.9 jit_solution(14853509759460529215)
XLA Ops:
  5.2 6.3 %all-to-all-start.1 = ((bf16[8,3,4,4096]{3,2,1,0:T(4,128)(2,1)}), bf16[8,3,4,4096]{3,2,1,0:T(4,128)(2,1)S(1)}, u32[]{:S(2)}, u32[]{:S(2)}) async-start(bf16[8,3,4,4096]{3,2,1,0:T(4,128)(2,1)} %copy.101), calls=%async_computation.1 | async-start | bytes 1572864 | tf_op jit(solution)/shard_map/all_to_all | solution.py:73
  13.3 19.1 %all-to-all-done.1 = bf16[8,3,4,4096]{3,2,1,0:T(4,128)(2,1)S(1)} async-done(((bf16[8,3,4,4096]{3,2,1,0:T(4,128)(2,1)}), bf16[8,3,4,4096]{3,2,1,0:T(4,128)(2,1)S(1)}, u32[]{:S(2)}, u32[]{:S(2)}) %all-to-all-start.1) | async-done | bytes 786464 | tf_op jit(solution)/shard_map/all_to_all | solution.py:73
  32.5 3.5 all-to-all-start
  41.7 15.3 %all-to-all-done = bf16[8,3,4,4096]{3,2,1,0:T(4,128)(2,1)S(1)} async-done(((bf16[8,3,4,4096]{3,2,1,0:T(4,128)(2,1)}), bf16[8,3,4,4096]{3,2,1,0:T(4,128)(2,1)S(1)}, u32[]{:S(2)}, u32[]{:S(2)}) %all-to-all-start) | async-done | bytes 786464 | tf_op jit(solution)/shard_map/all_to_all | solution.py:98
  57.1 3.8 fusion.69
  65.7 3.7 all-to-all-start.2
  72.2 18.1 %all-to-all-done.2 = bf16[8,3,4,4096]{3,2,1,0:T(4,128)(2,1)S(1)} async-done(((bf16[8,3,4,4096]{3,2,1,0:T(4,128)(2,1)}), bf16[8,3,4,4096]{3,2,1,0:T(4,128)(2,1)S(1)}, u32[]{:S(2)}, u32[]{:S(2)}) %all-to-all-start.2) | async-done | bytes 786464 | tf_op jit(solution)/shard_map/all_to_all | solution.py:102
  90.3 3.5 all-to-all-start.4
  98.5 9.4 %collective-permute-done = bf16[4,8,4096]{2,1,0:T(8,128)(2,1)S(1)} collective-permute-done((bf16[4,8,4096]{2,1,0:T(8,128)(2,1)}, bf16[4,8,4096]{2,1,0:T(8,128)(2,1)S(1)}, u32[]{:S(2)}, u32[]{:S(2)}) %collective-permute-start) | collective-permute-done | bytes 262176 | tf_op jit(solution)/shard_map/ppermute | solution.py:14
  109.7 5.0 all-to-all-done.4
  114.7 4.7 all-to-all-start.3
  125.5 14.9 %all-to-all-done.3 = bf16[8,3,4,4096]{3,2,1,0:T(4,128)(2,1)} async-done(((bf16[8,3,4,4096]{3,2,1,0:T(4,128)(2,1)}), bf16[8,3,4,4096]{3,2,1,0:T(4,128)(2,1)}, u32[]{:S(2)}, u32[]{:S(2)}) %all-to-all-start.3) | async-done | bytes 786464 | tf_op jit(solution)/shard_map/all_to_all | solution.py:98
  142.0 3.8 fusion.67
  150.5 3.5 all-to-all-start.5
  156.9 18.1 %all-to-all-done.5 = bf16[8,3,4,4096]{3,2,1,0:T(4,128)(2,1)S(1)} async-done(((bf16[8,3,4,4096]{3,2,1,0:T(4,128)(2,1)}), bf16[8,3,4,4096]{3,2,1,0:T(4,128)(2,1)S(1)}, u32[]{:S(2)}, u32[]{:S(2)}) %all-to-all-start.5) | async-done | bytes 786464 | tf_op jit(solution)/shard_map/all_to_all | solution.py:102
  175.8 3.5 all-to-all-start.7
  183.6 9.5 %collective-permute-done.1 = bf16[4,8,4096]{2,1,0:T(8,128)(2,1)} collective-permute-done((bf16[4,8,4096]{2,1,0:T(8,128)(2,1)}, bf16[4,8,4096]{2,1,0:T(8,128)(2,1)}, u32[]{:S(2)}, u32[]{:S(2)}) %collective-permute-start.1) | collective-permute-done | bytes 262176 | tf_op jit(solution)/shard_map/ppermute | solution.py:14
  195.9 4.3 all-to-all-done.7
  200.3 4.4 all-to-all-start.6
  210.5 15.1 %all-to-all-done.6 = bf16[8,3,4,4096]{3,2,1,0:T(4,128)(2,1)} async-done(((bf16[8,3,4,4096]{3,2,1,0:T(4,128)(2,1)}), bf16[8,3,4,4096]{3,2,1,0:T(4,128)(2,1)}, u32[]{:S(2)}, u32[]{:S(2)}) %all-to-all-start.6) | async-done | bytes 786464 | tf_op jit(solution)/shard_map/all_to_all | solution.py:98
  227.2 3.8 fusion.65
  235.8 3.5 all-to-all-start.8
  242.1 18.1 %all-to-all-done.8 = bf16[8,3,4,4096]{3,2,1,0:T(4,128)(2,1)S(1)} async-done(((bf16[8,3,4,4096]{3,2,1,0:T(4,128)(2,1)}), bf16[8,3,4,4096]{3,2,1,0:T(4,128)(2,1)S(1)}, u32[]{:S(2)}, u32[]{:S(2)}) %all-to-all-start.8) | async-done | bytes 786464 | tf_op jit(solution)/shard_map/all_to_all | solution.py:102
  268.9 9.5 %collective-permute-done.2 = bf16[4,8,4096]{2,1,0:T(8,128)(2,1)} collective-permute-done((bf16[4,8,4096]{2,1,0:T(8,128)(2,1)}, bf16[4,8,4096]{2,1,0:T(8,128)(2,1)}, u32[]{:S(2)}, u32[]{:S(2)}) %collective-permute-start.2) | collective-permute-done | bytes 262176 | tf_op jit(solution)/shard_map/ppermute | solution.py:14
  281.2 4.3 all-to-all-done.10
  285.6 4.4 all-to-all-start.9
  295.8 15.1 %all-to-all-done.9 = bf16[8,3,4,4096]{3,2,1,0:T(4,128)(2,1)} async-done(((bf16[8,3,4,4096]{3,2,1,0:T(4,128)(2,1)}), bf16[8,3,4,4096]{3,2,1,0:T(4,128)(2,1)}, u32[]{:S(2)}, u32[]{:S(2)}) %all-to-all-start.9) | async-done | bytes 786464 | tf_op jit(solution)/shard_map/all_to_all | solution.py:98
  312.5 3.8 fusion.63
  321.1 3.5 all-to-all-start.11
  324.6 20.9 %all-to-all-done.11 = bf16[8,3,4,4096]{3,2,1,0:T(4,128)(2,1)S(1)} async-done(((bf16[8,3,4,4096]{3,2,1,0:T(4,128)(2,1)}), bf16[8,3,4,4096]{3,2,1,0:T(4,128)(2,1)S(1)}, u32[]{:S(2)}, u32[]{:S(2)}) %all-to-all-start.11) | async-done | bytes 786464 | tf_op jit(solution)/shard_map/all_to_all | solution.py:102
  349.5 8.6 %collective-permute-done.3 = bf16[4,8,4096]{2,1,0:T(8,128)(2,1)S(1)} collective-permute-done((bf16[4,8,4096]{2,1,0:T(8,128)(2,1)}, bf16[4,8,4096]{2,1,0:T(8,128)(2,1)S(1)}, u32[]{:S(2)}, u32[]{:S(2)}) %collective-permute-start.3) | collective-permute-done | bytes 262176 | tf_op jit(solution)/shard_map/ppermute | solution.py:14
  360.0 4.2 all-to-all-start.12
  364.3 20.9 %all-to-all-done.12 = bf16[8,3,4,4096]{3,2,1,0:T(4,128)(2,1)} async-done(((bf16[8,3,4,4096]{3,2,1,0:T(4,128)(2,1)}), bf16[8,3,4,4096]{3,2,1,0:T(4,128)(2,1)}, u32[]{:S(2)}, u32[]{:S(2)}) %all-to-all-start.12) | async-done | bytes 786464 | tf_op jit(solution)/shard_map/all_to_all | solution.py:98
  386.8 3.8 fusion.61
  395.3 3.5 all-to-all-start.13
  398.9 20.9 %all-to-all-done.13 = bf16[8,3,4,4096]{3,2,1,0:T(4,128)(2,1)S(1)} async-done(((bf16[8,3,4,4096]{3,2,1,0:T(4,128)(2,1)}), bf16[8,3,4,4096]{3,2,1,0:T(4,128)(2,1)S(1)}, u32[]{:S(2)}, u32[]{:S(2)}) %all-to-all-start.13) | async-done | bytes 786464 | tf_op jit(solution)/shard_map/all_to_all | solution.py:102
  424.0 9.1 %collective-permute-done.4 = bf16[4,8,4096]{2,1,0:T(8,128)(2,1)S(1)} collective-permute-done((bf16[4,8,4096]{2,1,0:T(8,128)(2,1)}, bf16[4,8,4096]{2,1,0:T(8,128)(2,1)S(1)}, u32[]{:S(2)}, u32[]{:S(2)}) %collective-permute-start.4) | collective-permute-done | bytes 262176 | tf_op jit(solution)/shard_map/ppermute | solution.py:14
  434.9 4.2 all-to-all-start.14
  439.2 20.9 %all-to-all-done.14 = bf16[8,3,4,4096]{3,2,1,0:T(4,128)(2,1)} async-done(((bf16[8,3,4,4096]{3,2,1,0:T(4,128)(2,1)}), bf16[8,3,4,4096]{3,2,1,0:T(4,128)(2,1)}, u32[]{:S(2)}, u32[]{:S(2)}) %all-to-all-start.14) | async-done | bytes 786464 | tf_op jit(solution)/shard_map/all_to_all | solution.py:98
  461.7 3.8 fusion.59
  470.2 3.5 all-to-all-start.15
  473.8 20.9 %all-to-all-done.15 = bf16[8,3,4,4096]{3,2,1,0:T(4,128)(2,1)S(1)} async-done(((bf16[8,3,4,4096]{3,2,1,0:T(4,128)(2,1)}), bf16[8,3,4,4096]{3,2,1,0:T(4,128)(2,1)S(1)}, u32[]{:S(2)}, u32[]{:S(2)}) %all-to-all-start.15) | async-done | bytes 786464 | tf_op jit(solution)/shard_map/all_to_all | solution.py:102
  498.7 9.5 %collective-permute-done.5 = bf16[4,8,4096]{2,1,0:T(8,128)(2,1)S(1)} collective-permute-done((bf16[4,8,4096]{2,1,0:T(8,128)(2,1)}, bf16[4,8,4096]{2,1,0:T(8,128)(2,1)S(1)}, u32[]{:S(2)}, u32[]{:S(2)}) %collective-permute-start.5) | collective-permute-done | bytes 262176 | tf_op jit(solution)/shard_map/ppermute | solution.py:14
  510.1 4.2 all-to-all-start.16
  514.3 20.9 %all-to-all-done.16 = bf16[8,3,4,4096]{3,2,1,0:T(4,128)(2,1)} async-done(((bf16[8,3,4,4096]{3,2,1,0:T(4,128)(2,1)}), bf16[8,3,4,4096]{3,2,1,0:T(4,128)(2,1)}, u32[]{:S(2)}, u32[]{:S(2)}) %all-to-all-start.16) | async-done | bytes 786464 | tf_op jit(solution)/shard_map/all_to_all | solution.py:98
  536.8 3.8 fusion.57
  545.4 3.5 all-to-all-start.17
  548.9 20.9 %all-to-all-done.17 = bf16[8,3,4,4096]{3,2,1,0:T(4,128)(2,1)S(1)} async-done(((bf16[8,3,4,4096]{3,2,1,0:T(4,128)(2,1)}), bf16[8,3,4,4096]{3,2,1,0:T(4,128)(2,1)S(1)}, u32[]{:S(2)}, u32[]{:S(2)}) %all-to-all-start.17) | async-done | bytes 786464 | tf_op jit(solution)/shard_map/all_to_all | solution.py:102
  (164 shorter events, 129.3 us)
Async XLA Ops:
  0.0 11.5 %copy-start.18 = (bf16[16,8,4096]{2,1,0:T(8,128)(2,1)S(1)}, bf16[16,8,4096]{2,1,0:T(8,128)(2,1)}, u32[]{:S(2)}) copy-start(bf16[16,8,4096]{2,1,0:T(8,128)(2,1)} %param.29) | copy-start | bytes 3145732
  5.2 27.3 %all-to-all-start.1 = ((bf16[8,3,4,4096]{3,2,1,0:T(4,128)(2,1)}), bf16[8,3,4,4096]{3,2,1,0:T(4,128)(2,1)S(1)}, u32[]{:S(2)}, u32[]{:S(2)}) async-start(bf16[8,3,4,4096]{3,2,1,0:T(4,128)(2,1)} %copy.101), calls=%async_computation.1 | async-start | bytes 1572864 | tf_op jit(solution)/shard_map/all_to_all | solution.py:73
  32.5 24.5 %all-to-all-start = ((bf16[8,3,4,4096]{3,2,1,0:T(4,128)(2,1)}), bf16[8,3,4,4096]{3,2,1,0:T(4,128)(2,1)S(1)}, u32[]{:S(2)}, u32[]{:S(2)}) async-start(bf16[8,3,4,4096]{3,2,1,0:T(4,128)(2,1)} %copy.100), calls=%async_computation | async-start | bytes 1572864 | tf_op jit(solution)/shard_map/all_to_all | solution.py:98
  36.2 3.9 copy-start.7
  57.1 3.8 copy-start
  57.1 3.8 copy-start.24
  64.5 29.3 %copy-start.36 = (bf16[1,16,8,2]{1,3,2,0:T(2,128)(2,1)S(1)}, bf16[1,16,8,2]{1,3,2,0:T(2,128)(2,1)}, u32[]{:S(2)}) copy-start(bf16[1,16,8,2]{1,3,2,0:T(2,128)(2,1)} %param.25) | copy-start | bytes 1540
  65.7 28.2 %copy-start.29 = (s32[16,8,2,8]{0,3,2,1:T(8,128)S(1)}, s32[16,8,2,8]{0,3,2,1:T(8,128)}, u32[]{:S(2)}) copy-start(s32[16,8,2,8]{0,3,2,1:T(8,128)} %copy-done.28) | copy-start | bytes 24580
  65.7 24.6 %all-to-all-start.2 = ((bf16[8,3,4,4096]{3,2,1,0:T(4,128)(2,1)}), bf16[8,3,4,4096]{3,2,1,0:T(4,128)(2,1)S(1)}, u32[]{:S(2)}, u32[]{:S(2)}) async-start(bf16[8,3,4,4096]{3,2,1,0:T(4,128)(2,1)} %reshape.349), calls=%async_computation.2 | async-start | bytes 1572864 | tf_op jit(solution)/shard_map/all_to_all | solution.py:102
  90.3 24.5 %all-to-all-start.4 = ((bf16[8,3,4,4096]{3,2,1,0:T(4,128)(2,1)}), bf16[8,3,4,4096]{3,2,1,0:T(4,128)(2,1)S(1)}, u32[]{:S(2)}, u32[]{:S(2)}) async-start(bf16[8,3,4,4096]{3,2,1,0:T(4,128)(2,1)} %copy.104), calls=%async_computation.4 | async-start | bytes 1572864 | tf_op jit(solution)/shard_map/all_to_all | solution.py:73
  93.8 25.6 %copy-start.23 = (f32[1,96,512]{2,1,0:T(8,128)S(1)}, f32[1,96,512]{2,1,0:T(8,128)}, u32[]{:S(2)}) copy-start(f32[1,96,512]{2,1,0:T(8,128)} %multiply_bitcast_fusion) | copy-start | bytes 589828
  94.1 25.5 %copy-start.25 = (f32[1,96,512]{2,1,0:T(8,128)S(1)}, f32[1,96,512]{2,1,0:T(8,128)}, u32[]{:S(2)}) copy-start(f32[1,96,512]{2,1,0:T(8,128)} %fusion.74) | copy-start | bytes 589828
  97.2 10.7 %collective-permute-start = (bf16[4,8,4096]{2,1,0:T(8,128)(2,1)}, bf16[4,8,4096]{2,1,0:T(8,128)(2,1)S(1)}, u32[]{:S(2)}, u32[]{:S(2)}) collective-permute-start(bf16[4,8,4096]{2,1,0:T(8,128)(2,1)} %get-tuple-element.102), channel_id=1, source_target_pairs={{8,0},{16,8},{24,16},{9,1},{17,9},{25,17},{10,2},{18,10},{26,18},{... | collective-permute-start | bytes 786440 | tf_op jit(solution)/shard_map/ppermute | solution.py:14
  107.9 11.7 %copy-start.30 = (bf16[4,8,4096]{2,1,0:T(8,128)(2,1)}, bf16[4,8,4096]{2,1,0:T(8,128)(2,1)S(1)}, u32[]{:S(2)}) copy-start(bf16[4,8,4096]{2,1,0:T(8,128)(2,1)S(1)} %collective-permute-done) | copy-start | bytes 786436
  114.7 4.7 copy-start.19
  114.7 25.7 %all-to-all-start.3 = ((bf16[8,3,4,4096]{3,2,1,0:T(4,128)(2,1)}), bf16[8,3,4,4096]{3,2,1,0:T(4,128)(2,1)}, u32[]{:S(2)}, u32[]{:S(2)}) async-start(bf16[8,3,4,4096]{3,2,1,0:T(4,128)(2,1)} %copy.103), calls=%async_computation.3 | async-start | bytes 1572864 | tf_op jit(solution)/shard_map/all_to_all | solution.py:98
  121.2 3.5 copy-start.9
  142.0 3.8 copy-start.1
  150.5 24.5 %all-to-all-start.5 = ((bf16[8,3,4,4096]{3,2,1,0:T(4,128)(2,1)}), bf16[8,3,4,4096]{3,2,1,0:T(4,128)(2,1)S(1)}, u32[]{:S(2)}, u32[]{:S(2)}) async-start(bf16[8,3,4,4096]{3,2,1,0:T(4,128)(2,1)} %reshape.354), calls=%async_computation.5 | async-start | bytes 1572864 | tf_op jit(solution)/shard_map/all_to_all | solution.py:102
  175.8 24.4 %all-to-all-start.7 = ((bf16[8,3,4,4096]{3,2,1,0:T(4,128)(2,1)}), bf16[8,3,4,4096]{3,2,1,0:T(4,128)(2,1)S(1)}, u32[]{:S(2)}, u32[]{:S(2)}) async-start(bf16[8,3,4,4096]{3,2,1,0:T(4,128)(2,1)} %copy.107), calls=%async_computation.7 | async-start | bytes 1572864 | tf_op jit(solution)/shard_map/all_to_all | solution.py:73
  182.3 10.8 %collective-permute-start.1 = (bf16[4,8,4096]{2,1,0:T(8,128)(2,1)}, bf16[4,8,4096]{2,1,0:T(8,128)(2,1)}, u32[]{:S(2)}, u32[]{:S(2)}) collective-permute-start(bf16[4,8,4096]{2,1,0:T(8,128)(2,1)} %get-tuple-element.106), channel_id=1, source_target_pairs={{8,0},{16,8},{24,16},{9,1},{17,9},{25,17},{10,2},{18,10},{26,18},{... | collective-permute-start | bytes 786440 | tf_op jit(solution)/shard_map/ppermute | solution.py:14
  200.3 4.4 copy-start.20
  200.3 25.4 %all-to-all-start.6 = ((bf16[8,3,4,4096]{3,2,1,0:T(4,128)(2,1)}), bf16[8,3,4,4096]{3,2,1,0:T(4,128)(2,1)}, u32[]{:S(2)}, u32[]{:S(2)}) async-start(bf16[8,3,4,4096]{3,2,1,0:T(4,128)(2,1)} %copy.106), calls=%async_computation.6 | async-start | bytes 1572864 | tf_op jit(solution)/shard_map/all_to_all | solution.py:98
  206.3 3.5 copy-start.11
  227.2 3.8 copy-start.2
  235.8 24.5 %all-to-all-start.8 = ((bf16[8,3,4,4096]{3,2,1,0:T(4,128)(2,1)}), bf16[8,3,4,4096]{3,2,1,0:T(4,128)(2,1)S(1)}, u32[]{:S(2)}, u32[]{:S(2)}) async-start(bf16[8,3,4,4096]{3,2,1,0:T(4,128)(2,1)} %reshape.359), calls=%async_computation.8 | async-start | bytes 1572864 | tf_op jit(solution)/shard_map/all_to_all | solution.py:102
  261.1 24.4 %all-to-all-start.10 = ((bf16[8,3,4,4096]{3,2,1,0:T(4,128)(2,1)}), bf16[8,3,4,4096]{3,2,1,0:T(4,128)(2,1)S(1)}, u32[]{:S(2)}, u32[]{:S(2)}) async-start(bf16[8,3,4,4096]{3,2,1,0:T(4,128)(2,1)} %copy.110), calls=%async_computation.10 | async-start | bytes 1572864 | tf_op jit(solution)/shard_map/all_to_all | solution.py:73
  267.6 10.8 %collective-permute-start.2 = (bf16[4,8,4096]{2,1,0:T(8,128)(2,1)}, bf16[4,8,4096]{2,1,0:T(8,128)(2,1)}, u32[]{:S(2)}, u32[]{:S(2)}) collective-permute-start(bf16[4,8,4096]{2,1,0:T(8,128)(2,1)} %get-tuple-element.110), channel_id=1, source_target_pairs={{8,0},{16,8},{24,16},{9,1},{17,9},{25,17},{10,2},{18,10},{26,18},{... | collective-permute-start | bytes 786440 | tf_op jit(solution)/shard_map/ppermute | solution.py:14
  285.6 4.5 copy-start.21
  285.6 25.4 %all-to-all-start.9 = ((bf16[8,3,4,4096]{3,2,1,0:T(4,128)(2,1)}), bf16[8,3,4,4096]{3,2,1,0:T(4,128)(2,1)}, u32[]{:S(2)}, u32[]{:S(2)}) async-start(bf16[8,3,4,4096]{3,2,1,0:T(4,128)(2,1)} %copy.109), calls=%async_computation.9 | async-start | bytes 1572864 | tf_op jit(solution)/shard_map/all_to_all | solution.py:98
  312.5 3.8 copy-start.3
  321.1 24.5 %all-to-all-start.11 = ((bf16[8,3,4,4096]{3,2,1,0:T(4,128)(2,1)}), bf16[8,3,4,4096]{3,2,1,0:T(4,128)(2,1)S(1)}, u32[]{:S(2)}, u32[]{:S(2)}) async-start(bf16[8,3,4,4096]{3,2,1,0:T(4,128)(2,1)} %reshape.364), calls=%async_computation.11 | async-start | bytes 1572864 | tf_op jit(solution)/shard_map/all_to_all | solution.py:102
  348.2 9.9 %collective-permute-start.3 = (bf16[4,8,4096]{2,1,0:T(8,128)(2,1)}, bf16[4,8,4096]{2,1,0:T(8,128)(2,1)S(1)}, u32[]{:S(2)}, u32[]{:S(2)}) collective-permute-start(bf16[4,8,4096]{2,1,0:T(8,128)(2,1)} %get-tuple-element.114), channel_id=1, source_target_pairs={{8,0},{16,8},{24,16},{9,1},{17,9},{25,17},{10,2},{18,10},{26,18},{... | collective-permute-start | bytes 786440 | tf_op jit(solution)/shard_map/ppermute | solution.py:14
  358.2 6.1 %copy-start.34 = (bf16[4,8,4096]{2,1,0:T(8,128)(2,1)}, bf16[4,8,4096]{2,1,0:T(8,128)(2,1)S(1)}, u32[]{:S(2)}) copy-start(bf16[4,8,4096]{2,1,0:T(8,128)(2,1)S(1)} %collective-permute-done.3) | copy-start | bytes 786436
  360.0 25.2 %all-to-all-start.12 = ((bf16[8,3,4,4096]{3,2,1,0:T(4,128)(2,1)}), bf16[8,3,4,4096]{3,2,1,0:T(4,128)(2,1)}, u32[]{:S(2)}, u32[]{:S(2)}) async-start(bf16[8,3,4,4096]{3,2,1,0:T(4,128)(2,1)} %copy.112), calls=%async_computation.12 | async-start | bytes 1572864 | tf_op jit(solution)/shard_map/all_to_all | solution.py:98
  386.8 3.8 copy-start.4
  395.3 24.5 %all-to-all-start.13 = ((bf16[8,3,4,4096]{3,2,1,0:T(4,128)(2,1)}), bf16[8,3,4,4096]{3,2,1,0:T(4,128)(2,1)S(1)}, u32[]{:S(2)}, u32[]{:S(2)}) async-start(bf16[8,3,4,4096]{3,2,1,0:T(4,128)(2,1)} %reshape.366), calls=%async_computation.13 | async-start | bytes 1572864 | tf_op jit(solution)/shard_map/all_to_all | solution.py:102
  422.5 10.6 %collective-permute-start.4 = (bf16[4,8,4096]{2,1,0:T(8,128)(2,1)}, bf16[4,8,4096]{2,1,0:T(8,128)(2,1)S(1)}, u32[]{:S(2)}, u32[]{:S(2)}) collective-permute-start(bf16[4,8,4096]{2,1,0:T(8,128)(2,1)} %get-tuple-element.116), channel_id=1, source_target_pairs={{8,0},{16,8},{24,16},{9,1},{17,9},{25,17},{10,2},{18,10},{26,18},{... | collective-permute-start | bytes 786440 | tf_op jit(solution)/shard_map/ppermute | solution.py:14
  433.1 6.1 %copy-start.33 = (bf16[4,8,4096]{2,1,0:T(8,128)(2,1)}, bf16[4,8,4096]{2,1,0:T(8,128)(2,1)S(1)}, u32[]{:S(2)}) copy-start(bf16[4,8,4096]{2,1,0:T(8,128)(2,1)S(1)} %collective-permute-done.4) | copy-start | bytes 786436
  434.9 25.2 %all-to-all-start.14 = ((bf16[8,3,4,4096]{3,2,1,0:T(4,128)(2,1)}), bf16[8,3,4,4096]{3,2,1,0:T(4,128)(2,1)}, u32[]{:S(2)}, u32[]{:S(2)}) async-start(bf16[8,3,4,4096]{3,2,1,0:T(4,128)(2,1)} %copy.114), calls=%async_computation.14 | async-start | bytes 1572864 | tf_op jit(solution)/shard_map/all_to_all | solution.py:98
  461.7 3.8 copy-start.5
  470.2 24.5 %all-to-all-start.15 = ((bf16[8,3,4,4096]{3,2,1,0:T(4,128)(2,1)}), bf16[8,3,4,4096]{3,2,1,0:T(4,128)(2,1)S(1)}, u32[]{:S(2)}, u32[]{:S(2)}) async-start(bf16[8,3,4,4096]{3,2,1,0:T(4,128)(2,1)} %reshape.368), calls=%async_computation.15 | async-start | bytes 1572864 | tf_op jit(solution)/shard_map/all_to_all | solution.py:102
  497.4 10.8 %collective-permute-start.5 = (bf16[4,8,4096]{2,1,0:T(8,128)(2,1)}, bf16[4,8,4096]{2,1,0:T(8,128)(2,1)S(1)}, u32[]{:S(2)}, u32[]{:S(2)}) collective-permute-start(bf16[4,8,4096]{2,1,0:T(8,128)(2,1)} %get-tuple-element.118), channel_id=1, source_target_pairs={{8,0},{16,8},{24,16},{9,1},{17,9},{25,17},{10,2},{18,10},{26,18},{... | collective-permute-start | bytes 786440 | tf_op jit(solution)/shard_map/ppermute | solution.py:14
  508.2 6.1 %copy-start.31 = (bf16[4,8,4096]{2,1,0:T(8,128)(2,1)}, bf16[4,8,4096]{2,1,0:T(8,128)(2,1)S(1)}, u32[]{:S(2)}) copy-start(bf16[4,8,4096]{2,1,0:T(8,128)(2,1)S(1)} %collective-permute-done.5) | copy-start | bytes 786436
  510.1 25.2 %all-to-all-start.16 = ((bf16[8,3,4,4096]{3,2,1,0:T(4,128)(2,1)}), bf16[8,3,4,4096]{3,2,1,0:T(4,128)(2,1)}, u32[]{:S(2)}, u32[]{:S(2)}) async-start(bf16[8,3,4,4096]{3,2,1,0:T(4,128)(2,1)} %copy.116), calls=%async_computation.16 | async-start | bytes 1572864 | tf_op jit(solution)/shard_map/all_to_all | solution.py:98
  536.8 3.8 copy-start.6
  542.8 27.0 %copy-start.32 = (bf16[4,8,4096]{2,1,0:T(8,128)(2,1)S(1)}, bf16[4,8,4096]{2,1,0:T(8,128)(2,1)}, u32[]{:S(2)}) copy-start(bf16[4,8,4096]{2,1,0:T(8,128)(2,1)} %copy-done.31) | copy-start | bytes 786436
  545.4 24.5 %all-to-all-start.17 = ((bf16[8,3,4,4096]{3,2,1,0:T(4,128)(2,1)}), bf16[8,3,4,4096]{3,2,1,0:T(4,128)(2,1)S(1)}, u32[]{:S(2)}, u32[]{:S(2)}) async-start(bf16[8,3,4,4096]{3,2,1,0:T(4,128)(2,1)} %reshape.370), calls=%async_computation.17 | async-start | bytes 1572864 | tf_op jit(solution)/shard_map/all_to_all | solution.py:102
  (13 other events, 27.2 us)
where the time goes:
time: 585 us; the launch traced here: 575 us
  waiting for transfers between devices  350 us (60%)
  matrix products  89.9 us (15%)
  starting transfers between devices  79.5 us (14%)
  local copies, waits for them, and re-layouts  51.3 us (9%)
    all_to_all x7, waiting for transfers between devices, tick(): lax.all_to_all(back.reshape(expert_count, capacity, chunk, model_width),...  138 us
    all_to_all x7, waiting for transfers between devices, tick(): lax.all_to_all(grad_rows, 'expert', split_axis=0, concat_axis=0, tiled=True)  123 us
    ppermute x6, waiting for transfers between devices, passed_along(): return lax.ppermute(x, axis, pairs)  55.6 us
    all_to_all x4, waiting for transfers between devices, forward_chunk(): lax.all_to_all(outgoing, 'expert', split_axis=0, concat_axis=0, tiled=True)  32.9 us
    all_to_all x7, starting transfers between devices, tick(): lax.all_to_all(grad_rows, 'expert', split_axis=0, concat_axis=0, tiled=True)  29.7 us
    dot_general x7, matrix products, backward_rows(): down_grad = jnp.dot(grad_block, down_t, preferred_element_type=jnp.float32)  26.3 us
    all_to_all x7, starting transfers between devices, tick(): lax.all_to_all(back.reshape(expert_count, capacity, chunk, model_width),...  25 us
    dot_general x7, matrix products, tick(): jnp.einsum('mtec,ekcmd->mtd', combine_chunk, returned, preferred_element_...  18.1 us
  transfers between devices with their start and end apart: 24, of which 24 were waited for; matrix products, arithmetic and copies ran while one was open for 9% of the time, Pallas kernels for 0%

commit v1 on v0

--- a/solution.py
+++ b/solution.py
@@ -81,7 +81,7 @@
 
     def tick(tick_index, state_pair):
         incoming, results, act_all, coef_all = state_pair
-        if tick_index < chunk_count:
+        if isinstance(tick_index, int):
             act_new, coef_new = forward_chunk(tick_index * chunk)
             act_all = act_all.at[tick_index].set(act_new)
             coef_all = coef_all.at[tick_index].set(coef_new)
@@ -123,8 +123,11 @@
         jnp.zeros((chunk_count, expert_count * chunk * capacity, hidden), jnp.float32),
     )
     final_state = initial
-    for tick_index in range(chunk_count + section_count - 1):
+    for tick_index in range(chunk_count):
         final_state = tick(tick_index, final_state)
+    final_state = lax.fori_loop(
+        chunk_count, chunk_count + section_count - 1, tick, final_state
+    )
     return final_state[1][chunk : chunk + micro_count][None]
 
 

time: 585 us -> 588 us (level)
    ppermute x6 -> x7, waiting for transfers between devices: 55.6 us -> 57.7 us  [passed_along(): return lax.ppermute(x, axis, pairs)]
  transfers between devices with their start and end apart: 24 -> 25, of which waited for: 24 -> 25; matrix products, arithmetic and copies ran while one was open for 9% -> 9% of each run, Pallas kernels for 0% -> 0%
where the time goes in v1:
time: 588 us; the launch traced here: 577 us
  waiting for transfers between devices  355 us (60%)
  matrix products  92.6 us (16%)
  starting transfers between devices  78.2 us (13%)
  local copies, waits for them, and re-layouts  48.2 us (8%)
    all_to_all x7, waiting for transfers between devices, tick(): lax.all_to_all(back.reshape(expert_count, capacity, chunk, model_width),...  138 us
    all_to_all x7, waiting for transfers between devices, tick(): lax.all_to_all(grad_rows, 'expert', split_axis=0, concat_axis=0, tiled=True)  128 us
    ppermute x7, waiting for transfers between devices, passed_along(): return lax.ppermute(x, axis, pairs)  57.7 us
    all_to_all x4, waiting for transfers between devices, forward_chunk(): lax.all_to_all(outgoing, 'expert', split_axis=0, concat_axis=0, tiled=True)  30.7 us
    all_to_all x7, starting transfers between devices, tick(): lax.all_to_all(grad_rows, 'expert', split_axis=0, concat_axis=0, tiled=True)  27.5 us
    all_to_all x7, starting transfers between devices, tick(): lax.all_to_all(back.reshape(expert_count, capacity, chunk, model_width),...  24.8 us
    dot_general x7, matrix products, backward_rows(): down_grad = jnp.dot(grad_block, down_t, preferred_element_type=jnp.float32)  24.4 us
    dot_general x7, matrix products, tick(): jnp.einsum('mtec,ekcmd->mtd', combine_chunk, returned, preferred_element_...  18.5 us
  transfers between devices with their start and end apart: 25, of which 25 were waited for; matrix products, arithmetic and copies ran while one was open for 9% of the time, Pallas kernels for 0%

profile of v1, /device:TPU:0, one launch (start us, length us, event | category | flops | bytes accessed | tf_op | source)
XLA Modules:
  0.0 577.4 jit_solution(5811963795939359458)
XLA Ops:
  5.0 6.3 %all-to-all-start.3 = ((bf16[8,3,4,4096]{3,2,1,0:T(4,128)(2,1)}), bf16[8,3,4,4096]{3,2,1,0:T(4,128)(2,1)S(1)}, u32[]{:S(2)}, u32[]{:S(2)}) async-start(bf16[8,3,4,4096]{3,2,1,0:T(4,128)(2,1)} %copy.90), calls=%async_computation.3 | async-start | bytes 1572864 | tf_op jit(solution)/shard_map/all_to_all | solution.py:73
  14.1 18.2 %all-to-all-done.3 = bf16[8,3,4,4096]{3,2,1,0:T(4,128)(2,1)S(1)} async-done(((bf16[8,3,4,4096]{3,2,1,0:T(4,128)(2,1)}), bf16[8,3,4,4096]{3,2,1,0:T(4,128)(2,1)S(1)}, u32[]{:S(2)}, u32[]{:S(2)}) %all-to-all-start.3) | async-done | bytes 786464 | tf_op jit(solution)/shard_map/all_to_all | solution.py:73
  32.3 3.5 all-to-all-start.2
  40.4 16.4 %all-to-all-done.2 = bf16[8,3,4,4096]{3,2,1,0:T(4,128)(2,1)S(1)} async-done(((bf16[8,3,4,4096]{3,2,1,0:T(4,128)(2,1)}), bf16[8,3,4,4096]{3,2,1,0:T(4,128)(2,1)S(1)}, u32[]{:S(2)}, u32[]{:S(2)}) %all-to-all-start.2) | async-done | bytes 786464 | tf_op jit(solution)/shard_map/all_to_all | solution.py:98
  57.0 3.8 fusion.37
  65.5 3.5 all-to-all-start.4
  71.9 18.1 %all-to-all-done.4 = bf16[8,3,4,4096]{3,2,1,0:T(4,128)(2,1)S(1)} async-done(((bf16[8,3,4,4096]{3,2,1,0:T(4,128)(2,1)}), bf16[8,3,4,4096]{3,2,1,0:T(4,128)(2,1)S(1)}, u32[]{:S(2)}, u32[]{:S(2)}) %all-to-all-start.4) | async-done | bytes 786464 | tf_op jit(solution)/shard_map/all_to_all | solution.py:102
  90.0 3.5 all-to-all-start.6
  99.0 9.2 %collective-permute-done.1 = bf16[4,8,4096]{2,1,0:T(8,128)(2,1)S(1)} collective-permute-done((bf16[4,8,4096]{2,1,0:T(8,128)(2,1)S(1)}, bf16[4,8,4096]{2,1,0:T(8,128)(2,1)S(1)}, u32[]{:S(2)}, u32[]{:S(2)}) %collective-permute-start.1) | collective-permute-done | bytes 262176 | tf_op jit(solution)/shard_map/ppermute | solution.py:14
  111.1 3.3 all-to-all-done.6
  114.4 4.4 all-to-all-start.5
  123.5 16.3 %all-to-all-done.5 = bf16[8,3,4,4096]{3,2,1,0:T(4,128)(2,1)} async-done(((bf16[8,3,4,4096]{3,2,1,0:T(4,128)(2,1)}), bf16[8,3,4,4096]{3,2,1,0:T(4,128)(2,1)}, u32[]{:S(2)}, u32[]{:S(2)}) %all-to-all-start.5) | async-done | bytes 786464 | tf_op jit(solution)/shard_map/all_to_all | solution.py:98
  141.4 3.8 fusion.35
  149.9 3.5 all-to-all-start.7
  156.3 18.1 %all-to-all-done.7 = bf16[8,3,4,4096]{3,2,1,0:T(4,128)(2,1)S(1)} async-done(((bf16[8,3,4,4096]{3,2,1,0:T(4,128)(2,1)}), bf16[8,3,4,4096]{3,2,1,0:T(4,128)(2,1)S(1)}, u32[]{:S(2)}, u32[]{:S(2)}) %all-to-all-start.7) | async-done | bytes 786464 | tf_op jit(solution)/shard_map/all_to_all | solution.py:102
  174.4 3.5 all-to-all-start.9
  182.0 9.4 %collective-permute-done.2 = bf16[4,8,4096]{2,1,0:T(8,128)(2,1)S(1)} collective-permute-done((bf16[4,8,4096]{2,1,0:T(8,128)(2,1)}, bf16[4,8,4096]{2,1,0:T(8,128)(2,1)S(1)}, u32[]{:S(2)}, u32[]{:S(2)}) %collective-permute-start.2) | collective-permute-done | bytes 262176 | tf_op jit(solution)/shard_map/ppermute | solution.py:14
  194.3 4.6 all-to-all-done.9
  198.8 4.4 all-to-all-start.8
  207.7 16.5 %all-to-all-done.8 = bf16[8,3,4,4096]{3,2,1,0:T(4,128)(2,1)} async-done(((bf16[8,3,4,4096]{3,2,1,0:T(4,128)(2,1)}), bf16[8,3,4,4096]{3,2,1,0:T(4,128)(2,1)}, u32[]{:S(2)}, u32[]{:S(2)}) %all-to-all-start.8) | async-done | bytes 786464 | tf_op jit(solution)/shard_map/all_to_all | solution.py:98
  225.8 3.8 fusion.33
  234.3 3.5 all-to-all-start.10
  240.7 18.1 %all-to-all-done.10 = bf16[8,3,4,4096]{3,2,1,0:T(4,128)(2,1)S(1)} async-done(((bf16[8,3,4,4096]{3,2,1,0:T(4,128)(2,1)}), bf16[8,3,4,4096]{3,2,1,0:T(4,128)(2,1)S(1)}, u32[]{:S(2)}, u32[]{:S(2)}) %all-to-all-start.10) | async-done | bytes 786464 | tf_op jit(solution)/shard_map/all_to_all | solution.py:102
  258.8 3.5 all-to-all-start.12
  266.4 9.4 %collective-permute-done.3 = bf16[4,8,4096]{2,1,0:T(8,128)(2,1)S(1)} collective-permute-done((bf16[4,8,4096]{2,1,0:T(8,128)(2,1)}, bf16[4,8,4096]{2,1,0:T(8,128)(2,1)S(1)}, u32[]{:S(2)}, u32[]{:S(2)}) %collective-permute-start.3) | collective-permute-done | bytes 262176 | tf_op jit(solution)/shard_map/ppermute | solution.py:14
  278.7 4.6 all-to-all-done.12
  283.2 4.5 all-to-all-start.11
  292.2 16.5 %all-to-all-done.11 = bf16[8,3,4,4096]{3,2,1,0:T(4,128)(2,1)} async-done(((bf16[8,3,4,4096]{3,2,1,0:T(4,128)(2,1)}), bf16[8,3,4,4096]{3,2,1,0:T(4,128)(2,1)}, u32[]{:S(2)}, u32[]{:S(2)}) %all-to-all-start.11) | async-done | bytes 786464 | tf_op jit(solution)/shard_map/all_to_all | solution.py:98
  310.3 3.8 fusion.31
  318.8 3.5 all-to-all-start.13
  322.4 20.9 %all-to-all-done.13 = bf16[8,3,4,4096]{3,2,1,0:T(4,128)(2,1)S(1)} async-done(((bf16[8,3,4,4096]{3,2,1,0:T(4,128)(2,1)}), bf16[8,3,4,4096]{3,2,1,0:T(4,128)(2,1)S(1)}, u32[]{:S(2)}, u32[]{:S(2)}) %all-to-all-start.13) | async-done | bytes 786464 | tf_op jit(solution)/shard_map/all_to_all | solution.py:102
  347.1 6.5 %copy.89 = bf16[1,512,4096]{1,2,0:T(8,128)(2,1)} copy(bf16[1,512,4096]{2,1,0:T(8,128)(2,1)} %param.30) | data formatting | bytes 8388608 | tf_op args[5]
  355.6 219.0 %while.25 = (s32[]{:T(128)}, bf16[4,8,4096]{2,1,0:T(8,128)(2,1)S(1)}, bf16[24,8,4096]{2,1,0:T(8,128)(2,1)}, pred[]{:T(512)}, s32[]{:T(128)}, /*index=5*/bf16[16,...) while((s32[]{:T(128)}, ...), condition=%wide.region_5.6_spmd, body=%wide.region_4.5_spmd.sunk | while | flops 1222574080 | bytes 65523900 | solution.py:128
  358.4 3.5 all-to-all-start
  362.0 20.9 %all-to-all-done = bf16[8,3,4,4096]{3,2,1,0:T(4,128)(2,1)S(1)} async-done(((bf16[8,3,4,4096]{3,2,1,0:T(4,128)(2,1)}), bf16[8,3,4,4096]{3,2,1,0:T(4,128)(2,1)S(1)}, u32[]{:S(2)}, u32[]{:S(2)}) %all-to-all-start) | async-done | bytes 786464 | tf_op jit(solution)/shard_map/while/body/eval_jaxpr/all_to_all | solution.py:98
  391.0 3.5 all-to-all-start.1
  394.5 20.9 %all-to-all-done.1 = bf16[8,3,4,4096]{3,2,1,0:T(4,128)(2,1)S(1)} async-done(((bf16[8,3,4,4096]{3,2,1,0:T(4,128)(2,1)}), bf16[8,3,4,4096]{3,2,1,0:T(4,128)(2,1)S(1)}, u32[]{:S(2)}, u32[]{:S(2)}) %all-to-all-start.1) | async-done | bytes 786464 | tf_op jit(solution)/shard_map/while/body/eval_jaxpr/all_to_all | solution.py:102
  419.3 9.1 %collective-permute-done = bf16[4,8,4096]{2,1,0:T(8,128)(2,1)S(1)} collective-permute-done((bf16[4,8,4096]{2,1,0:T(8,128)(2,1)S(1)}, bf16[4,8,4096]{2,1,0:T(8,128)(2,1)S(1)}, u32[]{:S(2)}, u32[]{:S(2)}) %collective-permute-start) | collective-permute-done | bytes 262176 | tf_op jit(solution)/shard_map/while/body/eval_jaxpr/ppermute | solution.py:14
  431.2 3.5 all-to-all-start
  434.8 20.9 %all-to-all-done = bf16[8,3,4,4096]{3,2,1,0:T(4,128)(2,1)S(1)} async-done(((bf16[8,3,4,4096]{3,2,1,0:T(4,128)(2,1)}), bf16[8,3,4,4096]{3,2,1,0:T(4,128)(2,1)S(1)}, u32[]{:S(2)}, u32[]{:S(2)}) %all-to-all-start) | async-done | bytes 786464 | tf_op jit(solution)/shard_map/while/body/eval_jaxpr/all_to_all | solution.py:98
  463.9 3.5 all-to-all-start.1
  467.4 20.9 %all-to-all-done.1 = bf16[8,3,4,4096]{3,2,1,0:T(4,128)(2,1)S(1)} async-done(((bf16[8,3,4,4096]{3,2,1,0:T(4,128)(2,1)}), bf16[8,3,4,4096]{3,2,1,0:T(4,128)(2,1)S(1)}, u32[]{:S(2)}, u32[]{:S(2)}) %all-to-all-start.1) | async-done | bytes 786464 | tf_op jit(solution)/shard_map/while/body/eval_jaxpr/all_to_all | solution.py:102
  492.2 9.3 %collective-permute-done = bf16[4,8,4096]{2,1,0:T(8,128)(2,1)S(1)} collective-permute-done((bf16[4,8,4096]{2,1,0:T(8,128)(2,1)S(1)}, bf16[4,8,4096]{2,1,0:T(8,128)(2,1)S(1)}, u32[]{:S(2)}, u32[]{:S(2)}) %collective-permute-start) | collective-permute-done | bytes 262176 | tf_op jit(solution)/shard_map/while/body/eval_jaxpr/ppermute | solution.py:14
  504.3 3.5 all-to-all-start
  507.9 20.9 %all-to-all-done = bf16[8,3,4,4096]{3,2,1,0:T(4,128)(2,1)S(1)} async-done(((bf16[8,3,4,4096]{3,2,1,0:T(4,128)(2,1)}), bf16[8,3,4,4096]{3,2,1,0:T(4,128)(2,1)S(1)}, u32[]{:S(2)}, u32[]{:S(2)}) %all-to-all-start) | async-done | bytes 786464 | tf_op jit(solution)/shard_map/while/body/eval_jaxpr/all_to_all | solution.py:98
  536.9 3.5 all-to-all-start.1
  540.5 20.9 %all-to-all-done.1 = bf16[8,3,4,4096]{3,2,1,0:T(4,128)(2,1)S(1)} async-done(((bf16[8,3,4,4096]{3,2,1,0:T(4,128)(2,1)}), bf16[8,3,4,4096]{3,2,1,0:T(4,128)(2,1)S(1)}, u32[]{:S(2)}, u32[]{:S(2)}) %all-to-all-start.1) | async-done | bytes 786464 | tf_op jit(solution)/shard_map/while/body/eval_jaxpr/all_to_all | solution.py:102
  565.3 9.3 %collective-permute-done = bf16[4,8,4096]{2,1,0:T(8,128)(2,1)S(1)} collective-permute-done((bf16[4,8,4096]{2,1,0:T(8,128)(2,1)S(1)}, bf16[4,8,4096]{2,1,0:T(8,128)(2,1)S(1)}, u32[]{:S(2)}, u32[]{:S(2)}) %collective-permute-start) | collective-permute-done | bytes 262176 | tf_op jit(solution)/shard_map/while/body/eval_jaxpr/ppermute | solution.py:14
  (146 shorter events, 132.4 us)
Async XLA Ops:
  5.0 27.3 %all-to-all-start.3 = ((bf16[8,3,4,4096]{3,2,1,0:T(4,128)(2,1)}), bf16[8,3,4,4096]{3,2,1,0:T(4,128)(2,1)S(1)}, u32[]{:S(2)}, u32[]{:S(2)}) async-start(bf16[8,3,4,4096]{3,2,1,0:T(4,128)(2,1)} %copy.90), calls=%async_computation.3 | async-start | bytes 1572864 | tf_op jit(solution)/shard_map/all_to_all | solution.py:73
  32.3 24.5 %all-to-all-start.2 = ((bf16[8,3,4,4096]{3,2,1,0:T(4,128)(2,1)}), bf16[8,3,4,4096]{3,2,1,0:T(4,128)(2,1)S(1)}, u32[]{:S(2)}, u32[]{:S(2)}) async-start(bf16[8,3,4,4096]{3,2,1,0:T(4,128)(2,1)} %copy.88), calls=%async_computation.2 | async-start | bytes 1572864 | tf_op jit(solution)/shard_map/all_to_all | solution.py:98
  36.1 3.5 copy-start.5
  57.0 3.8 copy-start
  60.8 2.2 copy-start.6
  64.4 29.2 %copy-start.21 = (bf16[1,16,8,2]{1,3,2,0:T(2,128)(2,1)S(1)}, bf16[1,16,8,2]{1,3,2,0:T(2,128)(2,1)}, u32[]{:S(2)}) copy-start(bf16[1,16,8,2]{1,3,2,0:T(2,128)(2,1)} %param.27) | copy-start | bytes 1540
  65.5 24.5 %all-to-all-start.4 = ((bf16[8,3,4,4096]{3,2,1,0:T(4,128)(2,1)}), bf16[8,3,4,4096]{3,2,1,0:T(4,128)(2,1)S(1)}, u32[]{:S(2)}, u32[]{:S(2)}) async-start(bf16[8,3,4,4096]{3,2,1,0:T(4,128)(2,1)} %reshape.347), calls=%async_computation.4 | async-start | bytes 1572864 | tf_op jit(solution)/shard_map/all_to_all | solution.py:102
  90.0 24.5 %all-to-all-start.6 = ((bf16[8,3,4,4096]{3,2,1,0:T(4,128)(2,1)}), bf16[8,3,4,4096]{3,2,1,0:T(4,128)(2,1)S(1)}, u32[]{:S(2)}, u32[]{:S(2)}) async-start(bf16[8,3,4,4096]{3,2,1,0:T(4,128)(2,1)} %copy.93), calls=%async_computation.6 | async-start | bytes 1572864 | tf_op jit(solution)/shard_map/all_to_all | solution.py:73
  93.7 4.0 copy-start.20
  97.7 10.5 %collective-permute-start.1 = (bf16[4,8,4096]{2,1,0:T(8,128)(2,1)S(1)}, bf16[4,8,4096]{2,1,0:T(8,128)(2,1)S(1)}, u32[]{:S(2)}, u32[]{:S(2)}) collective-permute-start(bf16[4,8,4096]{2,1,0:T(8,128)(2,1)S(1)} %get-tuple-element.431), channel_id=1, source_target_pairs={{8,0},{16,8},{24,16},{9,1},{17,9},{25,17},{10,2},{18,10},{26,18},{... | collective-permute-start | bytes 786440 | tf_op jit(solution)/shard_map/ppermute | solution.py:14
  108.2 10.6 %copy-start.14 = (bf16[4,8,4096]{2,1,0:T(8,128)(2,1)}, bf16[4,8,4096]{2,1,0:T(8,128)(2,1)S(1)}, u32[]{:S(2)}) copy-start(bf16[4,8,4096]{2,1,0:T(8,128)(2,1)S(1)} %collective-permute-done.1) | copy-start | bytes 786436
  114.4 25.4 %all-to-all-start.5 = ((bf16[8,3,4,4096]{3,2,1,0:T(4,128)(2,1)}), bf16[8,3,4,4096]{3,2,1,0:T(4,128)(2,1)}, u32[]{:S(2)}, u32[]{:S(2)}) async-start(bf16[8,3,4,4096]{3,2,1,0:T(4,128)(2,1)} %copy.92), calls=%async_computation.5 | async-start | bytes 1572864 | tf_op jit(solution)/shard_map/all_to_all | solution.py:98
  119.2 3.5 copy-start.7
  141.4 3.8 copy-start.1
  148.7 29.2 %copy-start.15 = (bf16[4,8,4096]{2,1,0:T(8,128)(2,1)S(1)}, bf16[4,8,4096]{2,1,0:T(8,128)(2,1)}, u32[]{:S(2)}) copy-start(bf16[4,8,4096]{2,1,0:T(8,128)(2,1)} %copy-done.14) | copy-start | bytes 786436
  149.9 24.5 %all-to-all-start.7 = ((bf16[8,3,4,4096]{3,2,1,0:T(4,128)(2,1)}), bf16[8,3,4,4096]{3,2,1,0:T(4,128)(2,1)S(1)}, u32[]{:S(2)}, u32[]{:S(2)}) async-start(bf16[8,3,4,4096]{3,2,1,0:T(4,128)(2,1)} %reshape.352), calls=%async_computation.7 | async-start | bytes 1572864 | tf_op jit(solution)/shard_map/all_to_all | solution.py:102
  174.4 24.5 %all-to-all-start.9 = ((bf16[8,3,4,4096]{3,2,1,0:T(4,128)(2,1)}), bf16[8,3,4,4096]{3,2,1,0:T(4,128)(2,1)S(1)}, u32[]{:S(2)}, u32[]{:S(2)}) async-start(bf16[8,3,4,4096]{3,2,1,0:T(4,128)(2,1)} %copy.96), calls=%async_computation.9 | async-start | bytes 1572864 | tf_op jit(solution)/shard_map/all_to_all | solution.py:73
  180.7 10.7 %collective-permute-start.2 = (bf16[4,8,4096]{2,1,0:T(8,128)(2,1)}, bf16[4,8,4096]{2,1,0:T(8,128)(2,1)S(1)}, u32[]{:S(2)}, u32[]{:S(2)}) collective-permute-start(bf16[4,8,4096]{2,1,0:T(8,128)(2,1)} %get-tuple-element.433), channel_id=1, source_target_pairs={{8,0},{16,8},{24,16},{9,1},{17,9},{25,17},{10,2},{18,10},{26,18},{... | collective-permute-start | bytes 786440 | tf_op jit(solution)/shard_map/ppermute | solution.py:14
  191.4 11.9 %copy-start.16 = (bf16[4,8,4096]{2,1,0:T(8,128)(2,1)}, bf16[4,8,4096]{2,1,0:T(8,128)(2,1)S(1)}, u32[]{:S(2)}) copy-start(bf16[4,8,4096]{2,1,0:T(8,128)(2,1)S(1)} %collective-permute-done.2) | copy-start | bytes 786436
  198.8 25.4 %all-to-all-start.8 = ((bf16[8,3,4,4096]{3,2,1,0:T(4,128)(2,1)}), bf16[8,3,4,4096]{3,2,1,0:T(4,128)(2,1)}, u32[]{:S(2)}, u32[]{:S(2)}) async-start(bf16[8,3,4,4096]{3,2,1,0:T(4,128)(2,1)} %copy.95), calls=%async_computation.8 | async-start | bytes 1572864 | tf_op jit(solution)/shard_map/all_to_all | solution.py:98
  203.5 3.5 copy-start.9
  225.8 3.8 copy-start.2
  233.2 29.2 %copy-start.17 = (bf16[4,8,4096]{2,1,0:T(8,128)(2,1)S(1)}, bf16[4,8,4096]{2,1,0:T(8,128)(2,1)}, u32[]{:S(2)}) copy-start(bf16[4,8,4096]{2,1,0:T(8,128)(2,1)} %copy-done.16) | copy-start | bytes 786436
  234.3 24.5 %all-to-all-start.10 = ((bf16[8,3,4,4096]{3,2,1,0:T(4,128)(2,1)}), bf16[8,3,4,4096]{3,2,1,0:T(4,128)(2,1)S(1)}, u32[]{:S(2)}, u32[]{:S(2)}) async-start(bf16[8,3,4,4096]{3,2,1,0:T(4,128)(2,1)} %reshape.357), calls=%async_computation.10 | async-start | bytes 1572864 | tf_op jit(solution)/shard_map/all_to_all | solution.py:102
  258.8 24.5 %all-to-all-start.12 = ((bf16[8,3,4,4096]{3,2,1,0:T(4,128)(2,1)}), bf16[8,3,4,4096]{3,2,1,0:T(4,128)(2,1)S(1)}, u32[]{:S(2)}, u32[]{:S(2)}) async-start(bf16[8,3,4,4096]{3,2,1,0:T(4,128)(2,1)} %copy.99), calls=%async_computation.12 | async-start | bytes 1572864 | tf_op jit(solution)/shard_map/all_to_all | solution.py:73
  265.1 10.7 %collective-permute-start.3 = (bf16[4,8,4096]{2,1,0:T(8,128)(2,1)}, bf16[4,8,4096]{2,1,0:T(8,128)(2,1)S(1)}, u32[]{:S(2)}, u32[]{:S(2)}) collective-permute-start(bf16[4,8,4096]{2,1,0:T(8,128)(2,1)} %get-tuple-element.435), channel_id=1, source_target_pairs={{8,0},{16,8},{24,16},{9,1},{17,9},{25,17},{10,2},{18,10},{26,18},{... | collective-permute-start | bytes 786440 | tf_op jit(solution)/shard_map/ppermute | solution.py:14
  275.8 12.0 %copy-start.18 = (bf16[4,8,4096]{2,1,0:T(8,128)(2,1)}, bf16[4,8,4096]{2,1,0:T(8,128)(2,1)S(1)}, u32[]{:S(2)}) copy-start(bf16[4,8,4096]{2,1,0:T(8,128)(2,1)S(1)} %collective-permute-done.3) | copy-start | bytes 786436
  283.2 25.4 %all-to-all-start.11 = ((bf16[8,3,4,4096]{3,2,1,0:T(4,128)(2,1)}), bf16[8,3,4,4096]{3,2,1,0:T(4,128)(2,1)}, u32[]{:S(2)}, u32[]{:S(2)}) async-start(bf16[8,3,4,4096]{3,2,1,0:T(4,128)(2,1)} %copy.98), calls=%async_computation.11 | async-start | bytes 1572864 | tf_op jit(solution)/shard_map/all_to_all | solution.py:98
  287.9 3.5 copy-start.11
  310.3 3.8 copy-start.3
  316.2 27.0 %copy-start.19 = (bf16[4,8,4096]{2,1,0:T(8,128)(2,1)S(1)}, bf16[4,8,4096]{2,1,0:T(8,128)(2,1)}, u32[]{:S(2)}) copy-start(bf16[4,8,4096]{2,1,0:T(8,128)(2,1)} %copy-done.18) | copy-start | bytes 786436
  318.8 24.5 %all-to-all-start.13 = ((bf16[8,3,4,4096]{3,2,1,0:T(4,128)(2,1)}), bf16[8,3,4,4096]{3,2,1,0:T(4,128)(2,1)S(1)}, u32[]{:S(2)}, u32[]{:S(2)}) async-start(bf16[8,3,4,4096]{3,2,1,0:T(4,128)(2,1)} %reshape.362), calls=%async_computation.13 | async-start | bytes 1572864 | tf_op jit(solution)/shard_map/all_to_all | solution.py:102
  345.8 9.7 %collective-permute-start.4 = (bf16[4,8,4096]{2,1,0:T(8,128)(2,1)S(1)}, bf16[4,8,4096]{2,1,0:T(8,128)(2,1)S(1)}, u32[]{:S(2)}, u32[]{:S(2)}) collective-permute-start(bf16[4,8,4096]{2,1,0:T(8,128)(2,1)S(1)} %get-tuple-element.437), channel_id=1, source_target_pairs={{8,0},{16,8},{24,16},{9,1},{17,9},{25,17},{10,2},{18,10},{26,18},{... | collective-permute-start | bytes 786440 | tf_op jit(solution)/shard_map/ppermute | solution.py:14
  358.4 24.5 %all-to-all-start = ((bf16[8,3,4,4096]{3,2,1,0:T(4,128)(2,1)}), bf16[8,3,4,4096]{3,2,1,0:T(4,128)(2,1)S(1)}, u32[]{:S(2)}, u32[]{:S(2)}) async-start(bf16[8,3,4,4096]{3,2,1,0:T(4,128)(2,1)} %copy.144), calls=%async_computation | async-start | bytes 1572864 | tf_op jit(solution)/shard_map/while/body/eval_jaxpr/all_to_all | solution.py:98
  383.0 3.5 copy-start.4
  386.1 2.3 copy-start.13
  391.0 24.5 %all-to-all-start.1 = ((bf16[8,3,4,4096]{3,2,1,0:T(4,128)(2,1)}), bf16[8,3,4,4096]{3,2,1,0:T(4,128)(2,1)S(1)}, u32[]{:S(2)}, u32[]{:S(2)}) async-start(bf16[8,3,4,4096]{3,2,1,0:T(4,128)(2,1)} %reshape.381), calls=%async_computation.1 | async-start | bytes 1572864 | tf_op jit(solution)/shard_map/while/body/eval_jaxpr/all_to_all | solution.py:102
  418.0 10.4 %collective-permute-start = (bf16[4,8,4096]{2,1,0:T(8,128)(2,1)S(1)}, bf16[4,8,4096]{2,1,0:T(8,128)(2,1)S(1)}, u32[]{:S(2)}, u32[]{:S(2)}) collective-permute-start(bf16[4,8,4096]{2,1,0:T(8,128)(2,1)S(1)} %get-tuple-element.519), channel_id=1, source_target_pairs={{8,0},{16,8},{24,16},{9,1},{17,9},{25,17},{10,2},{18,10},{26,18},{... | collective-permute-start | bytes 786440 | tf_op jit(solution)/shard_map/while/body/eval_jaxpr/ppermute | solution.py:14
  431.2 24.5 %all-to-all-start = ((bf16[8,3,4,4096]{3,2,1,0:T(4,128)(2,1)}), bf16[8,3,4,4096]{3,2,1,0:T(4,128)(2,1)S(1)}, u32[]{:S(2)}, u32[]{:S(2)}) async-start(bf16[8,3,4,4096]{3,2,1,0:T(4,128)(2,1)} %copy.144), calls=%async_computation | async-start | bytes 1572864 | tf_op jit(solution)/shard_map/while/body/eval_jaxpr/all_to_all | solution.py:98
  455.9 3.5 copy-start.4
  459.0 2.3 copy-start.13
  463.9 24.5 %all-to-all-start.1 = ((bf16[8,3,4,4096]{3,2,1,0:T(4,128)(2,1)}), bf16[8,3,4,4096]{3,2,1,0:T(4,128)(2,1)S(1)}, u32[]{:S(2)}, u32[]{:S(2)}) async-start(bf16[8,3,4,4096]{3,2,1,0:T(4,128)(2,1)} %reshape.381), calls=%async_computation.1 | async-start | bytes 1572864 | tf_op jit(solution)/shard_map/while/body/eval_jaxpr/all_to_all | solution.py:102
  490.9 10.6 %collective-permute-start = (bf16[4,8,4096]{2,1,0:T(8,128)(2,1)S(1)}, bf16[4,8,4096]{2,1,0:T(8,128)(2,1)S(1)}, u32[]{:S(2)}, u32[]{:S(2)}) collective-permute-start(bf16[4,8,4096]{2,1,0:T(8,128)(2,1)S(1)} %get-tuple-element.519), channel_id=1, source_target_pairs={{8,0},{16,8},{24,16},{9,1},{17,9},{25,17},{10,2},{18,10},{26,18},{... | collective-permute-start | bytes 786440 | tf_op jit(solution)/shard_map/while/body/eval_jaxpr/ppermute | solution.py:14
  504.3 24.5 %all-to-all-start = ((bf16[8,3,4,4096]{3,2,1,0:T(4,128)(2,1)}), bf16[8,3,4,4096]{3,2,1,0:T(4,128)(2,1)S(1)}, u32[]{:S(2)}, u32[]{:S(2)}) async-start(bf16[8,3,4,4096]{3,2,1,0:T(4,128)(2,1)} %copy.144), calls=%async_computation | async-start | bytes 1572864 | tf_op jit(solution)/shard_map/while/body/eval_jaxpr/all_to_all | solution.py:98
  529.0 3.5 copy-start.4
  532.1 2.3 copy-start.13
  536.9 24.5 %all-to-all-start.1 = ((bf16[8,3,4,4096]{3,2,1,0:T(4,128)(2,1)}), bf16[8,3,4,4096]{3,2,1,0:T(4,128)(2,1)S(1)}, u32[]{:S(2)}, u32[]{:S(2)}) async-start(bf16[8,3,4,4096]{3,2,1,0:T(4,128)(2,1)} %reshape.381), calls=%async_computation.1 | async-start | bytes 1572864 | tf_op jit(solution)/shard_map/while/body/eval_jaxpr/all_to_all | solution.py:102
  564.0 10.6 %collective-permute-start = (bf16[4,8,4096]{2,1,0:T(8,128)(2,1)S(1)}, bf16[4,8,4096]{2,1,0:T(8,128)(2,1)S(1)}, u32[]{:S(2)}, u32[]{:S(2)}) collective-permute-start(bf16[4,8,4096]{2,1,0:T(8,128)(2,1)S(1)} %get-tuple-element.519), channel_id=1, source_target_pairs={{8,0},{16,8},{24,16},{9,1},{17,9},{25,17},{10,2},{18,10},{26,18},{... | collective-permute-start | bytes 786440 | tf_op jit(solution)/shard_map/while/body/eval_jaxpr/ppermute | solution.py:14
  (3 other events, 6.6 us)

commit v2 on v0

--- a/solution.py
+++ b/solution.py
@@ -112,8 +112,8 @@
         )
         grad_in = (grad_out.astype(jnp.float32) + mixed).astype(jnp.bfloat16)
         slot = (jnp.clip(chunk_index, -1, chunk_count) + 1) * chunk
-        results = lax.dynamic_update_slice_in_dim(results, grad_in, slot, 0)
         passed = passed_along(grad_in, "section", -1)
+        results = lax.dynamic_update_slice_in_dim(results, lax.optimization_barrier(grad_in), slot, 0)
         return (passed, results, act_all, coef_all)
 
     initial = (

time: 585 us -> 583 us (level)
  blocking collectives: 0 us -> 70.4 us
  waiting for transfers between devices: 350 us -> 280 us
  starting transfers between devices: 79.5 us -> 68.7 us
  local copies, waits for them, and re-layouts: 51.3 us -> 59.9 us
    all_to_all x0 -> x3, blocking collectives: none -> 70.4 us  [tick(): lax.all_to_all(back.reshape(expert_count, capacity, chunk, model_width),...]
    all_to_all x7 -> x4, waiting for transfers between devices: 138 us -> 71.3 us  [tick(): lax.all_to_all(back.reshape(expert_count, capacity, chunk, model_width),...]
    all_to_all x7 -> x4, starting transfers between devices: 25 us -> 14.3 us  [tick(): lax.all_to_all(back.reshape(expert_count, capacity, chunk, model_width),...]
    dynamic_update_slice x0 -> x7, local copies, waits for them, and re-layouts: none -> 6.94 us  [tick(): lax.dynamic_update_slice_in_dim(results, lax.optimization_barrier(grad_in...]
  transfers between devices with their start and end apart: 24 -> 21, of which waited for: 24 -> 21; matrix products, arithmetic and copies ran while one was open for 9% -> 10% of each run, Pallas kernels for 0% -> 0%
where the time goes in v2:
time: 583 us; the launch traced here: 573 us
  waiting for transfers between devices  280 us (48%)
  matrix products  89.6 us (15%)
  blocking collectives  70.4 us (12%)
  starting transfers between devices  68.7 us (12%)
  local copies, waits for them, and re-layouts  59.9 us (10%)
    all_to_all x7, waiting for transfers between devices, tick(): lax.all_to_all(grad_rows, 'expert', split_axis=0, concat_axis=0, tiled=True)  119 us
    all_to_all x4, waiting for transfers between devices, tick(): lax.all_to_all(back.reshape(expert_count, capacity, chunk, model_width),...  71.3 us
    all_to_all x3, blocking collectives, tick(): lax.all_to_all(back.reshape(expert_count, capacity, chunk, model_width),...  70.4 us
    ppermute x6, waiting for transfers between devices, passed_along(): return lax.ppermute(x, axis, pairs)  54.7 us
    all_to_all x4, waiting for transfers between devices, forward_chunk(): lax.all_to_all(outgoing, 'expert', split_axis=0, concat_axis=0, tiled=True)  34.3 us
    all_to_all x7, starting transfers between devices, tick(): lax.all_to_all(grad_rows, 'expert', split_axis=0, concat_axis=0, tiled=True)  29.7 us
    dot_general x7, matrix products, backward_rows(): down_grad = jnp.dot(grad_block, down_t, preferred_element_type=jnp.float32)  26.3 us
    all_to_all x4, starting transfers between devices, forward_chunk(): lax.all_to_all(outgoing, 'expert', split_axis=0, concat_axis=0, tiled=True)  17 us
  transfers between devices with their start and end apart: 21, of which 21 were waited for; matrix products, arithmetic and copies ran while one was open for 10% of the time, Pallas kernels for 0%

profile of v2, /device:TPU:0, one launch (start us, length us, event | category | flops | bytes accessed | tf_op | source)
XLA Modules:
  0.0 573.0 jit_solution(15292808152257835450)
XLA Ops:
  5.2 6.3 %all-to-all-start.1 = ((bf16[8,3,4,4096]{3,2,1,0:T(4,128)(2,1)}), bf16[8,3,4,4096]{3,2,1,0:T(4,128)(2,1)S(1)}, u32[]{:S(2)}, u32[]{:S(2)}) async-start(bf16[8,3,4,4096]{3,2,1,0:T(4,128)(2,1)} %copy.101), calls=%async_computation.1 | async-start | bytes 1572864 | tf_op jit(solution)/shard_map/all_to_all | solution.py:73
  13.3 19.1 %all-to-all-done.1 = bf16[8,3,4,4096]{3,2,1,0:T(4,128)(2,1)S(1)} async-done(((bf16[8,3,4,4096]{3,2,1,0:T(4,128)(2,1)}), bf16[8,3,4,4096]{3,2,1,0:T(4,128)(2,1)S(1)}, u32[]{:S(2)}, u32[]{:S(2)}) %all-to-all-start.1) | async-done | bytes 786464 | tf_op jit(solution)/shard_map/all_to_all | solution.py:73
  32.5 3.5 all-to-all-start
  41.6 15.3 %all-to-all-done = bf16[8,3,4,4096]{3,2,1,0:T(4,128)(2,1)S(1)} async-done(((bf16[8,3,4,4096]{3,2,1,0:T(4,128)(2,1)}), bf16[8,3,4,4096]{3,2,1,0:T(4,128)(2,1)S(1)}, u32[]{:S(2)}, u32[]{:S(2)}) %all-to-all-start) | async-done | bytes 786464 | tf_op jit(solution)/shard_map/all_to_all | solution.py:98
  57.1 3.8 fusion.69
  65.7 3.7 all-to-all-start.2
  72.2 18.1 %all-to-all-done.2 = bf16[8,3,4,4096]{3,2,1,0:T(4,128)(2,1)S(1)} async-done(((bf16[8,3,4,4096]{3,2,1,0:T(4,128)(2,1)}), bf16[8,3,4,4096]{3,2,1,0:T(4,128)(2,1)S(1)}, u32[]{:S(2)}, u32[]{:S(2)}) %all-to-all-start.2) | async-done | bytes 786464 | tf_op jit(solution)/shard_map/all_to_all | solution.py:102
  90.3 3.5 all-to-all-start.4
  96.3 9.3 %collective-permute-done = bf16[4,8,4096]{2,1,0:T(8,128)(2,1)} collective-permute-done((bf16[4,8,4096]{2,1,0:T(8,128)(2,1)S(1)}, bf16[4,8,4096]{2,1,0:T(8,128)(2,1)}, u32[]{:S(2)}, u32[]{:S(2)}) %collective-permute-start) | collective-permute-done | bytes 262176 | tf_op jit(solution)/shard_map/ppermute | solution.py:14
  108.4 6.3 %all-to-all-done.4 = bf16[8,3,4,4096]{3,2,1,0:T(4,128)(2,1)S(1)} async-done(((bf16[8,3,4,4096]{3,2,1,0:T(4,128)(2,1)}), bf16[8,3,4,4096]{3,2,1,0:T(4,128)(2,1)S(1)}, u32[]{:S(2)}, u32[]{:S(2)}) %all-to-all-start.4) | async-done | bytes 786464 | tf_op jit(solution)/shard_map/all_to_all | solution.py:73
  114.7 4.7 all-to-all-start.3
  121.3 3.2 bitcast_dynamic-update-slice_fusion.2
  125.5 14.9 %all-to-all-done.3 = bf16[8,3,4,4096]{3,2,1,0:T(4,128)(2,1)} async-done(((bf16[8,3,4,4096]{3,2,1,0:T(4,128)(2,1)}), bf16[8,3,4,4096]{3,2,1,0:T(4,128)(2,1)}, u32[]{:S(2)}, u32[]{:S(2)}) %all-to-all-start.3) | async-done | bytes 786464 | tf_op jit(solution)/shard_map/all_to_all | solution.py:98
  142.0 3.8 fusion.67
  150.5 3.5 all-to-all-start.5
  156.9 18.1 %all-to-all-done.5 = bf16[8,3,4,4096]{3,2,1,0:T(4,128)(2,1)S(1)} async-done(((bf16[8,3,4,4096]{3,2,1,0:T(4,128)(2,1)}), bf16[8,3,4,4096]{3,2,1,0:T(4,128)(2,1)S(1)}, u32[]{:S(2)}, u32[]{:S(2)}) %all-to-all-start.5) | async-done | bytes 786464 | tf_op jit(solution)/shard_map/all_to_all | solution.py:102
  175.8 3.5 all-to-all-start.7
  183.5 9.5 %collective-permute-done.1 = bf16[4,8,4096]{2,1,0:T(8,128)(2,1)} collective-permute-done((bf16[4,8,4096]{2,1,0:T(8,128)(2,1)}, bf16[4,8,4096]{2,1,0:T(8,128)(2,1)}, u32[]{:S(2)}, u32[]{:S(2)}) %collective-permute-start.1) | collective-permute-done | bytes 262176 | tf_op jit(solution)/shard_map/ppermute | solution.py:14
  195.9 4.4 all-to-all-done.7
  200.3 4.4 all-to-all-start.6
  210.5 15.1 %all-to-all-done.6 = bf16[8,3,4,4096]{3,2,1,0:T(4,128)(2,1)} async-done(((bf16[8,3,4,4096]{3,2,1,0:T(4,128)(2,1)}), bf16[8,3,4,4096]{3,2,1,0:T(4,128)(2,1)}, u32[]{:S(2)}, u32[]{:S(2)}) %all-to-all-start.6) | async-done | bytes 786464 | tf_op jit(solution)/shard_map/all_to_all | solution.py:98
  227.2 3.8 fusion.65
  235.8 3.5 all-to-all-start.8
  242.1 18.1 %all-to-all-done.8 = bf16[8,3,4,4096]{3,2,1,0:T(4,128)(2,1)S(1)} async-done(((bf16[8,3,4,4096]{3,2,1,0:T(4,128)(2,1)}), bf16[8,3,4,4096]{3,2,1,0:T(4,128)(2,1)S(1)}, u32[]{:S(2)}, u32[]{:S(2)}) %all-to-all-start.8) | async-done | bytes 786464 | tf_op jit(solution)/shard_map/all_to_all | solution.py:102
  261.1 3.5 all-to-all-start.10
  268.8 9.5 %collective-permute-done.2 = bf16[4,8,4096]{2,1,0:T(8,128)(2,1)} collective-permute-done((bf16[4,8,4096]{2,1,0:T(8,128)(2,1)}, bf16[4,8,4096]{2,1,0:T(8,128)(2,1)}, u32[]{:S(2)}, u32[]{:S(2)}) %collective-permute-start.2) | collective-permute-done | bytes 262176 | tf_op jit(solution)/shard_map/ppermute | solution.py:14
  281.1 4.4 all-to-all-done.10
  285.5 4.4 all-to-all-start.9
  291.6 3.2 bitcast_dynamic-update-slice_fusion
  295.8 15.1 %all-to-all-done.9 = bf16[8,3,4,4096]{3,2,1,0:T(4,128)(2,1)} async-done(((bf16[8,3,4,4096]{3,2,1,0:T(4,128)(2,1)}), bf16[8,3,4,4096]{3,2,1,0:T(4,128)(2,1)}, u32[]{:S(2)}, u32[]{:S(2)}) %all-to-all-start.9) | async-done | bytes 786464 | tf_op jit(solution)/shard_map/all_to_all | solution.py:98
  312.5 3.8 fusion.63
  322.5 23.4 %all_to_all.90 = bf16[8,3,4,4096]{3,2,1,0:T(4,128)(2,1)S(1)} all-to-all(bf16[8,3,4,4096]{3,2,1,0:T(4,128)(2,1)S(1)} %reshape.364), channel_id=1, replica_groups=mesh['section'=4,'expert'=8] {'expert'}, dimensions={0} | all-to-all | bytes 1572864 | tf_op jit(solution)/shard_map/all_to_all | solution.py:102
  349.1 8.3 %collective-permute-done.3 = bf16[4,8,4096]{2,1,0:T(8,128)(2,1)S(1)} collective-permute-done((bf16[4,8,4096]{2,1,0:T(8,128)(2,1)S(1)}, bf16[4,8,4096]{2,1,0:T(8,128)(2,1)S(1)}, u32[]{:S(2)}, u32[]{:S(2)}) %collective-permute-start.3) | collective-permute-done | bytes 262176 | tf_op jit(solution)/shard_map/ppermute | solution.py:14
  359.2 4.2 all-to-all-start.12
  363.4 20.9 %all-to-all-done.12 = bf16[8,3,4,4096]{3,2,1,0:T(4,128)(2,1)} async-done(((bf16[8,3,4,4096]{3,2,1,0:T(4,128)(2,1)}), bf16[8,3,4,4096]{3,2,1,0:T(4,128)(2,1)}, u32[]{:S(2)}, u32[]{:S(2)}) %all-to-all-start.12) | async-done | bytes 786464 | tf_op jit(solution)/shard_map/all_to_all | solution.py:98
  385.9 3.8 fusion.61
  395.9 23.6 %all_to_all.91 = bf16[8,3,4,4096]{3,2,1,0:T(4,128)(2,1)S(1)} all-to-all(bf16[8,3,4,4096]{3,2,1,0:T(4,128)(2,1)S(1)} %reshape.366), channel_id=1, replica_groups=mesh['section'=4,'expert'=8] {'expert'}, dimensions={0} | all-to-all | bytes 1572864 | tf_op jit(solution)/shard_map/all_to_all | solution.py:102
  422.7 8.9 %collective-permute-done.4 = bf16[4,8,4096]{2,1,0:T(8,128)(2,1)S(1)} collective-permute-done((bf16[4,8,4096]{2,1,0:T(8,128)(2,1)S(1)}, bf16[4,8,4096]{2,1,0:T(8,128)(2,1)S(1)}, u32[]{:S(2)}, u32[]{:S(2)}) %collective-permute-start.4) | collective-permute-done | bytes 262176 | tf_op jit(solution)/shard_map/ppermute | solution.py:14
  433.5 4.2 all-to-all-start.14
  437.7 20.9 %all-to-all-done.14 = bf16[8,3,4,4096]{3,2,1,0:T(4,128)(2,1)} async-done(((bf16[8,3,4,4096]{3,2,1,0:T(4,128)(2,1)}), bf16[8,3,4,4096]{3,2,1,0:T(4,128)(2,1)}, u32[]{:S(2)}, u32[]{:S(2)}) %all-to-all-start.14) | async-done | bytes 786464 | tf_op jit(solution)/shard_map/all_to_all | solution.py:98
  460.3 3.8 fusion.59
  470.2 23.4 %all_to_all.92 = bf16[8,3,4,4096]{3,2,1,0:T(4,128)(2,1)S(1)} all-to-all(bf16[8,3,4,4096]{3,2,1,0:T(4,128)(2,1)S(1)} %reshape.368), channel_id=1, replica_groups=mesh['section'=4,'expert'=8] {'expert'}, dimensions={0} | all-to-all | bytes 1572864 | tf_op jit(solution)/shard_map/all_to_all | solution.py:102
  496.8 9.2 %collective-permute-done.5 = bf16[4,8,4096]{2,1,0:T(8,128)(2,1)S(1)} collective-permute-done((bf16[4,8,4096]{2,1,0:T(8,128)(2,1)S(1)}, bf16[4,8,4096]{2,1,0:T(8,128)(2,1)S(1)}, u32[]{:S(2)}, u32[]{:S(2)}) %collective-permute-start.5) | collective-permute-done | bytes 262176 | tf_op jit(solution)/shard_map/ppermute | solution.py:14
  507.8 4.2 all-to-all-start.16
  515.9 17.1 %all-to-all-done.16 = bf16[8,3,4,4096]{3,2,1,0:T(4,128)(2,1)} async-done(((bf16[8,3,4,4096]{3,2,1,0:T(4,128)(2,1)}), bf16[8,3,4,4096]{3,2,1,0:T(4,128)(2,1)}, u32[]{:S(2)}, u32[]{:S(2)}) %all-to-all-start.16) | async-done | bytes 786464 | tf_op jit(solution)/shard_map/all_to_all | solution.py:98
  534.6 3.8 fusion.57
  543.2 3.5 all-to-all-start.17
  550.5 17.1 %all-to-all-done.17 = bf16[8,3,4,4096]{3,2,1,0:T(4,128)(2,1)S(1)} async-done(((bf16[8,3,4,4096]{3,2,1,0:T(4,128)(2,1)}), bf16[8,3,4,4096]{3,2,1,0:T(4,128)(2,1)S(1)}, u32[]{:S(2)}, u32[]{:S(2)}) %all-to-all-start.17) | async-done | bytes 786464 | tf_op jit(solution)/shard_map/all_to_all | solution.py:102
  (180 shorter events, 127.5 us)
Async XLA Ops:
  0.0 11.5 %copy-start.18 = (bf16[16,8,4096]{2,1,0:T(8,128)(2,1)S(1)}, bf16[16,8,4096]{2,1,0:T(8,128)(2,1)}, u32[]{:S(2)}) copy-start(bf16[16,8,4096]{2,1,0:T(8,128)(2,1)} %param.29) | copy-start | bytes 3145732
  5.2 27.3 %all-to-all-start.1 = ((bf16[8,3,4,4096]{3,2,1,0:T(4,128)(2,1)}), bf16[8,3,4,4096]{3,2,1,0:T(4,128)(2,1)S(1)}, u32[]{:S(2)}, u32[]{:S(2)}) async-start(bf16[8,3,4,4096]{3,2,1,0:T(4,128)(2,1)} %copy.101), calls=%async_computation.1 | async-start | bytes 1572864 | tf_op jit(solution)/shard_map/all_to_all | solution.py:73
  32.5 24.5 %all-to-all-start = ((bf16[8,3,4,4096]{3,2,1,0:T(4,128)(2,1)}), bf16[8,3,4,4096]{3,2,1,0:T(4,128)(2,1)S(1)}, u32[]{:S(2)}, u32[]{:S(2)}) async-start(bf16[8,3,4,4096]{3,2,1,0:T(4,128)(2,1)} %copy.100), calls=%async_computation | async-start | bytes 1572864 | tf_op jit(solution)/shard_map/all_to_all | solution.py:98
  36.2 3.9 copy-start.7
  57.1 3.8 copy-start
  57.1 3.8 copy-start.24
  64.5 29.3 %copy-start.42 = (bf16[1,16,8,2]{1,3,2,0:T(2,128)(2,1)S(1)}, bf16[1,16,8,2]{1,3,2,0:T(2,128)(2,1)}, u32[]{:S(2)}) copy-start(bf16[1,16,8,2]{1,3,2,0:T(2,128)(2,1)} %param.25) | copy-start | bytes 1540
  65.7 28.2 %copy-start.29 = (s32[16,8,2,8]{0,3,2,1:T(8,128)S(1)}, s32[16,8,2,8]{0,3,2,1:T(8,128)}, u32[]{:S(2)}) copy-start(s32[16,8,2,8]{0,3,2,1:T(8,128)} %copy-done.28) | copy-start | bytes 24580
  65.7 24.6 %all-to-all-start.2 = ((bf16[8,3,4,4096]{3,2,1,0:T(4,128)(2,1)}), bf16[8,3,4,4096]{3,2,1,0:T(4,128)(2,1)S(1)}, u32[]{:S(2)}, u32[]{:S(2)}) async-start(bf16[8,3,4,4096]{3,2,1,0:T(4,128)(2,1)} %reshape.349), calls=%async_computation.2 | async-start | bytes 1572864 | tf_op jit(solution)/shard_map/all_to_all | solution.py:102
  72.2 47.2 %copy-start.23 = (f32[1,96,512]{2,1,0:T(8,128)S(1)}, f32[1,96,512]{2,1,0:T(8,128)}, u32[]{:S(2)}) copy-start(f32[1,96,512]{2,1,0:T(8,128)} %multiply_bitcast_fusion) | copy-start | bytes 589828
  72.2 47.4 %copy-start.25 = (f32[1,96,512]{2,1,0:T(8,128)S(1)}, f32[1,96,512]{2,1,0:T(8,128)}, u32[]{:S(2)}) copy-start(f32[1,96,512]{2,1,0:T(8,128)} %fusion.74) | copy-start | bytes 589828
  90.3 24.5 %all-to-all-start.4 = ((bf16[8,3,4,4096]{3,2,1,0:T(4,128)(2,1)}), bf16[8,3,4,4096]{3,2,1,0:T(4,128)(2,1)S(1)}, u32[]{:S(2)}, u32[]{:S(2)}) async-start(bf16[8,3,4,4096]{3,2,1,0:T(4,128)(2,1)} %copy.104), calls=%async_computation.4 | async-start | bytes 1572864 | tf_op jit(solution)/shard_map/all_to_all | solution.py:73
  94.0 25.5 %copy-start.41 = (bf16[16,8,8,3]{2,1,3,0:T(8,128)(2,1)}, bf16[16,8,8,3]{2,1,3,0:T(8,128)(2,1)S(1)}, u32[]{:S(2)}) copy-start(bf16[16,8,8,3]{2,1,3,0:T(8,128)(2,1)S(1)} %copy.98) | copy-start | bytes 18436
  95.0 24.6 %copy-start.30 = (bf16[4,8,4096]{2,1,0:T(8,128)(2,1)}, bf16[4,8,4096]{2,1,0:T(8,128)(2,1)S(1)}, u32[]{:S(2)}) copy-start(bf16[4,8,4096]{2,1,0:T(8,128)(2,1)S(1)} %fusion.19) | copy-start | bytes 786436
  95.0 10.6 %collective-permute-start = (bf16[4,8,4096]{2,1,0:T(8,128)(2,1)S(1)}, bf16[4,8,4096]{2,1,0:T(8,128)(2,1)}, u32[]{:S(2)}, u32[]{:S(2)}) collective-permute-start(bf16[4,8,4096]{2,1,0:T(8,128)(2,1)S(1)} %fusion.19), channel_id=1, source_target_pairs={{8,0},{16,8},{24,16},{9,1},{17,9},{25,17},{10,2},{18,10},{26,18},{... | collective-permute-start | bytes 786440 | tf_op jit(solution)/shard_map/ppermute | solution.py:14
  114.7 4.7 copy-start.19
  114.7 25.7 %all-to-all-start.3 = ((bf16[8,3,4,4096]{3,2,1,0:T(4,128)(2,1)}), bf16[8,3,4,4096]{3,2,1,0:T(4,128)(2,1)}, u32[]{:S(2)}, u32[]{:S(2)}) async-start(bf16[8,3,4,4096]{3,2,1,0:T(4,128)(2,1)} %copy.103), calls=%async_computation.3 | async-start | bytes 1572864 | tf_op jit(solution)/shard_map/all_to_all | solution.py:98
  142.0 3.8 copy-start.1
  150.5 24.5 %all-to-all-start.5 = ((bf16[8,3,4,4096]{3,2,1,0:T(4,128)(2,1)}), bf16[8,3,4,4096]{3,2,1,0:T(4,128)(2,1)S(1)}, u32[]{:S(2)}, u32[]{:S(2)}) async-start(bf16[8,3,4,4096]{3,2,1,0:T(4,128)(2,1)} %reshape.354), calls=%async_computation.5 | async-start | bytes 1572864 | tf_op jit(solution)/shard_map/all_to_all | solution.py:102
  175.8 24.4 %all-to-all-start.7 = ((bf16[8,3,4,4096]{3,2,1,0:T(4,128)(2,1)}), bf16[8,3,4,4096]{3,2,1,0:T(4,128)(2,1)S(1)}, u32[]{:S(2)}, u32[]{:S(2)}) async-start(bf16[8,3,4,4096]{3,2,1,0:T(4,128)(2,1)} %copy.107), calls=%async_computation.7 | async-start | bytes 1572864 | tf_op jit(solution)/shard_map/all_to_all | solution.py:73
  182.2 10.8 %collective-permute-start.1 = (bf16[4,8,4096]{2,1,0:T(8,128)(2,1)}, bf16[4,8,4096]{2,1,0:T(8,128)(2,1)}, u32[]{:S(2)}, u32[]{:S(2)}) collective-permute-start(bf16[4,8,4096]{2,1,0:T(8,128)(2,1)} %add_convert_fusion.5), channel_id=1, source_target_pairs={{8,0},{16,8},{24,16},{9,1},{17,9},{25,17},{10,2},{18,10},{26,18},{... | collective-permute-start | bytes 786440 | tf_op jit(solution)/shard_map/ppermute | solution.py:14
  200.3 4.4 copy-start.20
  200.3 25.4 %all-to-all-start.6 = ((bf16[8,3,4,4096]{3,2,1,0:T(4,128)(2,1)}), bf16[8,3,4,4096]{3,2,1,0:T(4,128)(2,1)}, u32[]{:S(2)}, u32[]{:S(2)}) async-start(bf16[8,3,4,4096]{3,2,1,0:T(4,128)(2,1)} %copy.106), calls=%async_computation.6 | async-start | bytes 1572864 | tf_op jit(solution)/shard_map/all_to_all | solution.py:98
  227.2 3.8 copy-start.2
  235.8 24.5 %all-to-all-start.8 = ((bf16[8,3,4,4096]{3,2,1,0:T(4,128)(2,1)}), bf16[8,3,4,4096]{3,2,1,0:T(4,128)(2,1)S(1)}, u32[]{:S(2)}, u32[]{:S(2)}) async-start(bf16[8,3,4,4096]{3,2,1,0:T(4,128)(2,1)} %reshape.359), calls=%async_computation.8 | async-start | bytes 1572864 | tf_op jit(solution)/shard_map/all_to_all | solution.py:102
  261.1 24.4 %all-to-all-start.10 = ((bf16[8,3,4,4096]{3,2,1,0:T(4,128)(2,1)}), bf16[8,3,4,4096]{3,2,1,0:T(4,128)(2,1)S(1)}, u32[]{:S(2)}, u32[]{:S(2)}) async-start(bf16[8,3,4,4096]{3,2,1,0:T(4,128)(2,1)} %copy.110), calls=%async_computation.10 | async-start | bytes 1572864 | tf_op jit(solution)/shard_map/all_to_all | solution.py:73
  267.5 10.8 %collective-permute-start.2 = (bf16[4,8,4096]{2,1,0:T(8,128)(2,1)}, bf16[4,8,4096]{2,1,0:T(8,128)(2,1)}, u32[]{:S(2)}, u32[]{:S(2)}) collective-permute-start(bf16[4,8,4096]{2,1,0:T(8,128)(2,1)} %add_convert_fusion.4), channel_id=1, source_target_pairs={{8,0},{16,8},{24,16},{9,1},{17,9},{25,17},{10,2},{18,10},{26,18},{... | collective-permute-start | bytes 786440 | tf_op jit(solution)/shard_map/ppermute | solution.py:14
  285.5 4.5 copy-start.21
  285.5 25.4 %all-to-all-start.9 = ((bf16[8,3,4,4096]{3,2,1,0:T(4,128)(2,1)}), bf16[8,3,4,4096]{3,2,1,0:T(4,128)(2,1)}, u32[]{:S(2)}, u32[]{:S(2)}) async-start(bf16[8,3,4,4096]{3,2,1,0:T(4,128)(2,1)} %copy.109), calls=%async_computation.9 | async-start | bytes 1572864 | tf_op jit(solution)/shard_map/all_to_all | solution.py:98
  312.5 3.8 copy-start.3
  347.8 15.7 %copy-start.32 = (bf16[4,8,4096]{2,1,0:T(8,128)(2,1)}, bf16[4,8,4096]{2,1,0:T(8,128)(2,1)S(1)}, u32[]{:S(2)}) copy-start(bf16[4,8,4096]{2,1,0:T(8,128)(2,1)S(1)} %add_convert_fusion.3) | copy-start | bytes 786436
  347.8 9.6 %collective-permute-start.3 = (bf16[4,8,4096]{2,1,0:T(8,128)(2,1)S(1)}, bf16[4,8,4096]{2,1,0:T(8,128)(2,1)S(1)}, u32[]{:S(2)}, u32[]{:S(2)}) collective-permute-start(bf16[4,8,4096]{2,1,0:T(8,128)(2,1)S(1)} %add_convert_fusion.3), channel_id=1, source_target_pairs={{8,0},{16,8},{24,16},{9,1},{17,9},{25,17},{10,2},{18,10},{26,18},{... | collective-permute-start | bytes 786440 | tf_op jit(solution)/shard_map/ppermute | solution.py:14
  357.3 6.1 %copy-start.40 = (bf16[4,8,4096]{2,1,0:T(8,128)(2,1)}, bf16[4,8,4096]{2,1,0:T(8,128)(2,1)S(1)}, u32[]{:S(2)}) copy-start(bf16[4,8,4096]{2,1,0:T(8,128)(2,1)S(1)} %collective-permute-done.3) | copy-start | bytes 786436
  359.2 25.2 %all-to-all-start.12 = ((bf16[8,3,4,4096]{3,2,1,0:T(4,128)(2,1)}), bf16[8,3,4,4096]{3,2,1,0:T(4,128)(2,1)}, u32[]{:S(2)}, u32[]{:S(2)}) async-start(bf16[8,3,4,4096]{3,2,1,0:T(4,128)(2,1)} %copy.112), calls=%async_computation.12 | async-start | bytes 1572864 | tf_op jit(solution)/shard_map/all_to_all | solution.py:98
  385.9 3.8 copy-start.4
  421.4 16.3 %copy-start.34 = (bf16[4,8,4096]{2,1,0:T(8,128)(2,1)}, bf16[4,8,4096]{2,1,0:T(8,128)(2,1)S(1)}, u32[]{:S(2)}) copy-start(bf16[4,8,4096]{2,1,0:T(8,128)(2,1)S(1)} %add_convert_fusion.2) | copy-start | bytes 786436
  421.4 10.2 %collective-permute-start.4 = (bf16[4,8,4096]{2,1,0:T(8,128)(2,1)S(1)}, bf16[4,8,4096]{2,1,0:T(8,128)(2,1)S(1)}, u32[]{:S(2)}, u32[]{:S(2)}) collective-permute-start(bf16[4,8,4096]{2,1,0:T(8,128)(2,1)S(1)} %add_convert_fusion.2), channel_id=1, source_target_pairs={{8,0},{16,8},{24,16},{9,1},{17,9},{25,17},{10,2},{18,10},{26,18},{... | collective-permute-start | bytes 786440 | tf_op jit(solution)/shard_map/ppermute | solution.py:14
  431.6 6.1 %copy-start.39 = (bf16[4,8,4096]{2,1,0:T(8,128)(2,1)}, bf16[4,8,4096]{2,1,0:T(8,128)(2,1)S(1)}, u32[]{:S(2)}) copy-start(bf16[4,8,4096]{2,1,0:T(8,128)(2,1)S(1)} %collective-permute-done.4) | copy-start | bytes 786436
  433.5 25.2 %all-to-all-start.14 = ((bf16[8,3,4,4096]{3,2,1,0:T(4,128)(2,1)}), bf16[8,3,4,4096]{3,2,1,0:T(4,128)(2,1)}, u32[]{:S(2)}, u32[]{:S(2)}) async-start(bf16[8,3,4,4096]{3,2,1,0:T(4,128)(2,1)} %copy.114), calls=%async_computation.14 | async-start | bytes 1572864 | tf_op jit(solution)/shard_map/all_to_all | solution.py:98
  493.6 19.9 %copy-start.31 = (bf16[4,8,4096]{2,1,0:T(8,128)(2,1)S(1)}, bf16[4,8,4096]{2,1,0:T(8,128)(2,1)}, u32[]{:S(2)}) copy-start(bf16[4,8,4096]{2,1,0:T(8,128)(2,1)} %copy-done.30) | copy-start | bytes 786436
  495.5 20.4 %copy-start.36 = (bf16[4,8,4096]{2,1,0:T(8,128)(2,1)}, bf16[4,8,4096]{2,1,0:T(8,128)(2,1)S(1)}, u32[]{:S(2)}) copy-start(bf16[4,8,4096]{2,1,0:T(8,128)(2,1)S(1)} %add_convert_fusion.1) | copy-start | bytes 786436
  495.5 10.5 %collective-permute-start.5 = (bf16[4,8,4096]{2,1,0:T(8,128)(2,1)S(1)}, bf16[4,8,4096]{2,1,0:T(8,128)(2,1)S(1)}, u32[]{:S(2)}, u32[]{:S(2)}) collective-permute-start(bf16[4,8,4096]{2,1,0:T(8,128)(2,1)S(1)} %add_convert_fusion.1), channel_id=1, source_target_pairs={{8,0},{16,8},{24,16},{9,1},{17,9},{25,17},{10,2},{18,10},{26,18},{... | collective-permute-start | bytes 786440 | tf_op jit(solution)/shard_map/ppermute | solution.py:14
  506.0 9.9 %copy-start.38 = (bf16[4,8,4096]{2,1,0:T(8,128)(2,1)}, bf16[4,8,4096]{2,1,0:T(8,128)(2,1)S(1)}, u32[]{:S(2)}) copy-start(bf16[4,8,4096]{2,1,0:T(8,128)(2,1)S(1)} %collective-permute-done.5) | copy-start | bytes 786436
  507.8 25.2 %all-to-all-start.16 = ((bf16[8,3,4,4096]{3,2,1,0:T(4,128)(2,1)}), bf16[8,3,4,4096]{3,2,1,0:T(4,128)(2,1)}, u32[]{:S(2)}, u32[]{:S(2)}) async-start(bf16[8,3,4,4096]{3,2,1,0:T(4,128)(2,1)} %copy.116), calls=%async_computation.16 | async-start | bytes 1572864 | tf_op jit(solution)/shard_map/all_to_all | solution.py:98
  540.6 7.8 %copy-start.33 = (bf16[4,8,4096]{2,1,0:T(8,128)(2,1)S(1)}, bf16[4,8,4096]{2,1,0:T(8,128)(2,1)}, u32[]{:S(2)}) copy-start(bf16[4,8,4096]{2,1,0:T(8,128)(2,1)} %copy-done.32) | copy-start | bytes 786436
  540.6 8.5 %copy-start.35 = (bf16[4,8,4096]{2,1,0:T(8,128)(2,1)S(1)}, bf16[4,8,4096]{2,1,0:T(8,128)(2,1)}, u32[]{:S(2)}) copy-start(bf16[4,8,4096]{2,1,0:T(8,128)(2,1)} %copy-done.34) | copy-start | bytes 786436
  540.6 9.2 %copy-start.37 = (bf16[4,8,4096]{2,1,0:T(8,128)(2,1)S(1)}, bf16[4,8,4096]{2,1,0:T(8,128)(2,1)}, u32[]{:S(2)}) copy-start(bf16[4,8,4096]{2,1,0:T(8,128)(2,1)} %copy-done.36) | copy-start | bytes 786436
  543.2 24.5 %all-to-all-start.17 = ((bf16[8,3,4,4096]{3,2,1,0:T(4,128)(2,1)}), bf16[8,3,4,4096]{3,2,1,0:T(4,128)(2,1)S(1)}, u32[]{:S(2)}, u32[]{:S(2)}) async-start(bf16[8,3,4,4096]{3,2,1,0:T(4,128)(2,1)} %reshape.370), calls=%async_computation.17 | async-start | bytes 1572864 | tf_op jit(solution)/shard_map/all_to_all | solution.py:102
  (16 other events, 38.5 us)

commit v3 on v2

--- a/solution.py
+++ b/solution.py
@@ -12,6 +12,15 @@
     length = lax.axis_size(axis)
     pairs = [(i, i + by) for i in range(length) if 0 <= i + by < length]
     return lax.ppermute(x, axis, pairs)
+
+
+def exchange(blocks, axis, direction):
+    count = blocks.shape[0]
+    moved = [blocks[0]]
+    for shift in range(1, count):
+        pairs = [(i, (i + direction * shift) % count) for i in range(count)]
+        moved.append(lax.ppermute(blocks[shift], axis, pairs))
+    return jnp.stack(moved)
 
 
 def selection(choices, capacity):
@@ -70,7 +79,14 @@
         outgoing = spread(
             jnp.einsum("mtec,mtd->ecmd", dispatch_part, inputs_chunk, preferred_element_type=jnp.float32)
         )
-        received = lax.all_to_all(outgoing, "expert", split_axis=0, concat_axis=0, tiled=True)
+        if first == 0:
+            index = lax.axis_index("expert")
+            places = jnp.arange(expert_count)
+            rotated = jnp.take(outgoing, (index + places) % expert_count, axis=0)
+            received = exchange(rotated, "expert", 1)
+            received = jnp.take(received, (index - places) % expert_count, axis=0)
+        else:
+            received = lax.all_to_all(outgoing, "expert", split_axis=0, concat_axis=0, tiled=True)
         row_block = received.reshape(-1, model_width)
         pre_gate = jnp.dot(row_block, gate_slice, preferred_element_type=jnp.float32)
         pre_up = jnp.dot(row_block, up_slice, preferred_element_type=jnp.float32)

time: 583 us -> 577 us (0.990)
  waiting for transfers between devices: 280 us -> 255 us
  starting transfers between devices: 68.7 us -> 81 us
  local copies, waits for them, and re-layouts: 59.9 us -> 65.9 us
    all_to_all x4 -> x3, waiting for transfers between devices: 34.3 us -> 14.5 us  [forward_chunk(): lax.all_to_all(outgoing, 'expert', split_axis=0, concat_axis=0, tiled=True)]
    all_to_all x7, waiting for transfers between devices: 119 us -> 104 us  [tick(): lax.all_to_all(grad_rows, 'expert', split_axis=0, concat_axis=0, tiled=True)]
    ppermute x0 -> x7, starting transfers between devices: none -> 12 us  [exchange(): moved.append(lax.ppermute(blocks[shift], axis, pairs))]
    ppermute x0 -> x7, waiting for transfers between devices: none -> 9.05 us  [exchange(): moved.append(lax.ppermute(blocks[shift], axis, pairs))]
    all_to_all x4, starting transfers between devices: 14.3 us -> 21.2 us  [tick(): lax.all_to_all(back.reshape(expert_count, capacity, chunk, model_width),...]
    all_to_all x4 -> x3, starting transfers between devices: 17 us -> 10.8 us  [forward_chunk(): lax.all_to_all(outgoing, 'expert', split_axis=0, concat_axis=0, tiled=True)]
    unnamed x86 -> x94, local copies, waits for them, and re-layouts: 8.28 us -> 12.1 us
  transfers between devices with their start and end apart: 21 -> 27, of which waited for: 21 -> 21; matrix products, arithmetic and copies ran while one was open for 10% -> 11% of each run, Pallas kernels for 0% -> 0%
where the time goes in v3:
time: 577 us; the launch traced here: 566 us
  waiting for transfers between devices  255 us (44%)
  matrix products  88.8 us (15%)
  starting transfers between devices  81 us (14%)
  blocking collectives  70.4 us (12%)
  local copies, waits for them, and re-layouts  65.9 us (11%)
    all_to_all x7, waiting for transfers between devices, tick(): lax.all_to_all(grad_rows, 'expert', split_axis=0, concat_axis=0, tiled=True)  104 us
    all_to_all x4, waiting for transfers between devices, tick(): lax.all_to_all(back.reshape(expert_count, capacity, chunk, model_width),...  71.2 us
    all_to_all x3, blocking collectives, tick(): lax.all_to_all(back.reshape(expert_count, capacity, chunk, model_width),...  70.4 us
    ppermute x6, waiting for transfers between devices, passed_along(): return lax.ppermute(x, axis, pairs)  56 us
    all_to_all x7, starting transfers between devices, tick(): lax.all_to_all(grad_rows, 'expert', split_axis=0, concat_axis=0, tiled=True)  29.4 us
    dot_general x7, matrix products, backward_rows(): down_grad = jnp.dot(grad_block, down_t, preferred_element_type=jnp.float32)  26.3 us
    all_to_all x4, starting transfers between devices, tick(): lax.all_to_all(back.reshape(expert_count, capacity, chunk, model_width),...  21.2 us
    convert_element_type x11, local copies, waits for them, and re-layouts, spread(): rows = rows.astype(jnp.bfloat16)  15.7 us
  transfers between devices with their start and end apart: 27, of which 21 were waited for; matrix products, arithmetic and copies ran while one was open for 11% of the time, Pallas kernels for 0%

profile of v3, /device:TPU:0, one launch (start us, length us, event | category | flops | bytes accessed | tf_op | source)
XLA Modules:
  0.0 566.3 jit_solution(14154430698867040459)
XLA Ops:
  16.3 3.5 all-to-all-start
  19.9 3.8 collective-permute-start.5
  27.7 8.7 %collective-permute-done.5 = bf16[3,4,4096]{2,1,0:T(4,128)(2,1)S(1)} collective-permute-done((bf16[3,4,4096]{2,1,0:T(4,128)(2,1)S(1)}, bf16[3,4,4096]{2,1,0:T(4,128)(2,1)S(1)}, u32[]{:S(2)}, u32[]{:S(2)}) %collective-permute-start.5) | collective-permute-done | bytes 98336 | tf_op jit(solution)/shard_map/ppermute | solution.py:22
  43.5 3.8 fusion.69
  52.1 10.5 %all-to-all-start.1 = ((bf16[8,3,4,4096]{3,2,1,0:T(4,128)(2,1)}), bf16[8,3,4,4096]{3,2,1,0:T(4,128)(2,1)S(1)}, u32[]{:S(2)}, u32[]{:S(2)}) async-start(bf16[8,3,4,4096]{3,2,1,0:T(4,128)(2,1)} %reshape.354), calls=%async_computation.1 | async-start | bytes 1572864 | tf_op jit(solution)/shard_map/all_to_all | solution.py:118
  65.5 18.1 %all-to-all-done.1 = bf16[8,3,4,4096]{3,2,1,0:T(4,128)(2,1)S(1)} async-done(((bf16[8,3,4,4096]{3,2,1,0:T(4,128)(2,1)}), bf16[8,3,4,4096]{3,2,1,0:T(4,128)(2,1)S(1)}, u32[]{:S(2)}, u32[]{:S(2)}) %all-to-all-start.1) | async-done | bytes 786464 | tf_op jit(solution)/shard_map/all_to_all | solution.py:118
  83.6 3.8 all-to-all-start.3
  89.8 9.6 %collective-permute-done.7 = bf16[4,8,4096]{2,1,0:T(8,128)(2,1)} collective-permute-done((bf16[4,8,4096]{2,1,0:T(8,128)(2,1)S(1)}, bf16[4,8,4096]{2,1,0:T(8,128)(2,1)}, u32[]{:S(2)}, u32[]{:S(2)}) %collective-permute-start.7) | collective-permute-done | bytes 262176 | tf_op jit(solution)/shard_map/ppermute | solution.py:14
  102.2 6.1 %all-to-all-done.3 = bf16[8,3,4,4096]{3,2,1,0:T(4,128)(2,1)S(1)} async-done(((bf16[8,3,4,4096]{3,2,1,0:T(4,128)(2,1)}), bf16[8,3,4,4096]{3,2,1,0:T(4,128)(2,1)S(1)}, u32[]{:S(2)}, u32[]{:S(2)}) %all-to-all-start.3) | async-done | bytes 786464 | tf_op jit(solution)/shard_map/all_to_all | solution.py:89
  108.3 4.2 all-to-all-start.2
  114.3 3.2 bitcast_dynamic-update-slice_fusion.2
  118.6 14.9 %all-to-all-done.2 = bf16[8,3,4,4096]{3,2,1,0:T(4,128)(2,1)} async-done(((bf16[8,3,4,4096]{3,2,1,0:T(4,128)(2,1)}), bf16[8,3,4,4096]{3,2,1,0:T(4,128)(2,1)}, u32[]{:S(2)}, u32[]{:S(2)}) %all-to-all-start.2) | async-done | bytes 786464 | tf_op jit(solution)/shard_map/all_to_all | solution.py:114
  135.0 3.8 fusion.67
  143.6 3.5 all-to-all-start.4
  150.0 18.0 %all-to-all-done.4 = bf16[8,3,4,4096]{3,2,1,0:T(4,128)(2,1)S(1)} async-done(((bf16[8,3,4,4096]{3,2,1,0:T(4,128)(2,1)}), bf16[8,3,4,4096]{3,2,1,0:T(4,128)(2,1)S(1)}, u32[]{:S(2)}, u32[]{:S(2)}) %all-to-all-start.4) | async-done | bytes 786464 | tf_op jit(solution)/shard_map/all_to_all | solution.py:118
  168.9 3.5 all-to-all-start.6
  176.6 9.8 %collective-permute-done.8 = bf16[4,8,4096]{2,1,0:T(8,128)(2,1)} collective-permute-done((bf16[4,8,4096]{2,1,0:T(8,128)(2,1)}, bf16[4,8,4096]{2,1,0:T(8,128)(2,1)}, u32[]{:S(2)}, u32[]{:S(2)}) %collective-permute-start.8) | collective-permute-done | bytes 262176 | tf_op jit(solution)/shard_map/ppermute | solution.py:14
  189.2 4.2 all-to-all-done.6
  193.4 4.6 all-to-all-start.5
  199.6 3.2 bitcast_dynamic-update-slice_fusion.1
  203.8 15.1 %all-to-all-done.5 = bf16[8,3,4,4096]{3,2,1,0:T(4,128)(2,1)} async-done(((bf16[8,3,4,4096]{3,2,1,0:T(4,128)(2,1)}), bf16[8,3,4,4096]{3,2,1,0:T(4,128)(2,1)}, u32[]{:S(2)}, u32[]{:S(2)}) %all-to-all-start.5) | async-done | bytes 786464 | tf_op jit(solution)/shard_map/all_to_all | solution.py:114
  220.5 3.8 fusion.65
  229.1 3.5 all-to-all-start.7
  235.5 18.0 %all-to-all-done.7 = bf16[8,3,4,4096]{3,2,1,0:T(4,128)(2,1)S(1)} async-done(((bf16[8,3,4,4096]{3,2,1,0:T(4,128)(2,1)}), bf16[8,3,4,4096]{3,2,1,0:T(4,128)(2,1)S(1)}, u32[]{:S(2)}, u32[]{:S(2)}) %all-to-all-start.7) | async-done | bytes 786464 | tf_op jit(solution)/shard_map/all_to_all | solution.py:118
  254.4 3.5 all-to-all-start.9
  262.1 9.8 %collective-permute-done.9 = bf16[4,8,4096]{2,1,0:T(8,128)(2,1)} collective-permute-done((bf16[4,8,4096]{2,1,0:T(8,128)(2,1)}, bf16[4,8,4096]{2,1,0:T(8,128)(2,1)}, u32[]{:S(2)}, u32[]{:S(2)}) %collective-permute-start.9) | collective-permute-done | bytes 262176 | tf_op jit(solution)/shard_map/ppermute | solution.py:14
  274.6 4.2 all-to-all-done.9
  278.8 4.4 all-to-all-start.8
  284.8 3.2 bitcast_dynamic-update-slice_fusion
  289.1 15.1 %all-to-all-done.8 = bf16[8,3,4,4096]{3,2,1,0:T(4,128)(2,1)} async-done(((bf16[8,3,4,4096]{3,2,1,0:T(4,128)(2,1)}), bf16[8,3,4,4096]{3,2,1,0:T(4,128)(2,1)}, u32[]{:S(2)}, u32[]{:S(2)}) %all-to-all-start.8) | async-done | bytes 786464 | tf_op jit(solution)/shard_map/all_to_all | solution.py:114
  305.8 3.8 fusion.63
  315.7 23.4 %all_to_all.85 = bf16[8,3,4,4096]{3,2,1,0:T(4,128)(2,1)S(1)} all-to-all(bf16[8,3,4,4096]{3,2,1,0:T(4,128)(2,1)S(1)} %reshape.369), channel_id=1, replica_groups=mesh['section'=4,'expert'=8] {'expert'}, dimensions={0} | all-to-all | bytes 1572864 | tf_op jit(solution)/shard_map/all_to_all | solution.py:118
  342.3 8.5 %collective-permute-done.10 = bf16[4,8,4096]{2,1,0:T(8,128)(2,1)S(1)} collective-permute-done((bf16[4,8,4096]{2,1,0:T(8,128)(2,1)S(1)}, bf16[4,8,4096]{2,1,0:T(8,128)(2,1)S(1)}, u32[]{:S(2)}, u32[]{:S(2)}) %collective-permute-start.10) | collective-permute-done | bytes 262176 | tf_op jit(solution)/shard_map/ppermute | solution.py:14
  352.7 4.2 all-to-all-start.11
  356.9 20.9 %all-to-all-done.11 = bf16[8,3,4,4096]{3,2,1,0:T(4,128)(2,1)} async-done(((bf16[8,3,4,4096]{3,2,1,0:T(4,128)(2,1)}), bf16[8,3,4,4096]{3,2,1,0:T(4,128)(2,1)}, u32[]{:S(2)}, u32[]{:S(2)}) %all-to-all-start.11) | async-done | bytes 786464 | tf_op jit(solution)/shard_map/all_to_all | solution.py:114
  379.4 3.8 fusion.61
  389.4 23.6 %all_to_all.86 = bf16[8,3,4,4096]{3,2,1,0:T(4,128)(2,1)S(1)} all-to-all(bf16[8,3,4,4096]{3,2,1,0:T(4,128)(2,1)S(1)} %reshape.371), channel_id=1, replica_groups=mesh['section'=4,'expert'=8] {'expert'}, dimensions={0} | all-to-all | bytes 1572864 | tf_op jit(solution)/shard_map/all_to_all | solution.py:118
  416.2 9.2 %collective-permute-done.11 = bf16[4,8,4096]{2,1,0:T(8,128)(2,1)S(1)} collective-permute-done((bf16[4,8,4096]{2,1,0:T(8,128)(2,1)S(1)}, bf16[4,8,4096]{2,1,0:T(8,128)(2,1)S(1)}, u32[]{:S(2)}, u32[]{:S(2)}) %collective-permute-start.11) | collective-permute-done | bytes 262176 | tf_op jit(solution)/shard_map/ppermute | solution.py:14
  427.2 4.2 all-to-all-start.13
  431.4 20.9 %all-to-all-done.13 = bf16[8,3,4,4096]{3,2,1,0:T(4,128)(2,1)} async-done(((bf16[8,3,4,4096]{3,2,1,0:T(4,128)(2,1)}), bf16[8,3,4,4096]{3,2,1,0:T(4,128)(2,1)}, u32[]{:S(2)}, u32[]{:S(2)}) %all-to-all-start.13) | async-done | bytes 786464 | tf_op jit(solution)/shard_map/all_to_all | solution.py:114
  453.9 3.8 fusion.59
  463.9 23.4 %all_to_all.87 = bf16[8,3,4,4096]{3,2,1,0:T(4,128)(2,1)S(1)} all-to-all(bf16[8,3,4,4096]{3,2,1,0:T(4,128)(2,1)S(1)} %reshape.373), channel_id=1, replica_groups=mesh['section'=4,'expert'=8] {'expert'}, dimensions={0} | all-to-all | bytes 1572864 | tf_op jit(solution)/shard_map/all_to_all | solution.py:118
  490.5 9.2 %collective-permute-done.12 = bf16[4,8,4096]{2,1,0:T(8,128)(2,1)S(1)} collective-permute-done((bf16[4,8,4096]{2,1,0:T(8,128)(2,1)S(1)}, bf16[4,8,4096]{2,1,0:T(8,128)(2,1)S(1)}, u32[]{:S(2)}, u32[]{:S(2)}) %collective-permute-start.12) | collective-permute-done | bytes 262176 | tf_op jit(solution)/shard_map/ppermute | solution.py:14
  501.5 4.2 all-to-all-start.15
  509.6 17.1 %all-to-all-done.15 = bf16[8,3,4,4096]{3,2,1,0:T(4,128)(2,1)} async-done(((bf16[8,3,4,4096]{3,2,1,0:T(4,128)(2,1)}), bf16[8,3,4,4096]{3,2,1,0:T(4,128)(2,1)}, u32[]{:S(2)}, u32[]{:S(2)}) %all-to-all-start.15) | async-done | bytes 786464 | tf_op jit(solution)/shard_map/all_to_all | solution.py:114
  528.3 3.8 fusion.57
  536.8 3.5 all-to-all-start.16
  544.3 17.0 %all-to-all-done.16 = bf16[8,3,4,4096]{3,2,1,0:T(4,128)(2,1)S(1)} async-done(((bf16[8,3,4,4096]{3,2,1,0:T(4,128)(2,1)}), bf16[8,3,4,4096]{3,2,1,0:T(4,128)(2,1)S(1)}, u32[]{:S(2)}, u32[]{:S(2)}) %all-to-all-start.16) | async-done | bytes 786464 | tf_op jit(solution)/shard_map/all_to_all | solution.py:118
  (212 shorter events, 138.8 us)
Async XLA Ops:
  2.3 12.2 %copy-start.18 = (bf16[16,8,4096]{2,1,0:T(8,128)(2,1)S(1)}, bf16[16,8,4096]{2,1,0:T(8,128)(2,1)}, u32[]{:S(2)}) copy-start(bf16[16,8,4096]{2,1,0:T(8,128)(2,1)} %param.31) | copy-start | bytes 3145732
  6.4 13.6 %collective-permute-start = (bf16[3,4,4096]{2,1,0:T(4,128)(2,1)S(1)}, bf16[3,4,4096]{2,1,0:T(4,128)(2,1)}, u32[]{:S(2)}, u32[]{:S(2)}) collective-permute-start(bf16[3,4,4096]{2,1,0:T(4,128)(2,1)S(1)} %get-tuple-element.108), channel_id=1, source_target_pairs={{0,1},{1,2},{2,3},{3,4},{4,5},{5,6},{6,7},{7,0},{8,9},{9,10},{10,1... | collective-permute-start | bytes 294920 | tf_op jit(solution)/shard_map/ppermute | solution.py:22
  6.9 17.8 %collective-permute-start.1 = (bf16[3,4,4096]{2,1,0:T(4,128)(2,1)S(1)}, bf16[3,4,4096]{2,1,0:T(4,128)(2,1)}, u32[]{:S(2)}, u32[]{:S(2)}) collective-permute-start(bf16[3,4,4096]{2,1,0:T(4,128)(2,1)S(1)} %get-tuple-element.107), channel_id=1, source_target_pairs={{0,2},{1,3},{2,4},{3,5},{4,6},{5,7},{6,0},{7,1},{8,10},{9,11},{10,... | collective-permute-start | bytes 294920 | tf_op jit(solution)/shard_map/ppermute | solution.py:22
  9.5 16.2 %collective-permute-start.2 = (bf16[3,4,4096]{2,1,0:T(4,128)(2,1)S(1)}, bf16[3,4,4096]{2,1,0:T(4,128)(2,1)}, u32[]{:S(2)}, u32[]{:S(2)}) collective-permute-start(bf16[3,4,4096]{2,1,0:T(4,128)(2,1)S(1)} %get-tuple-element.106), channel_id=1, source_target_pairs={{0,3},{1,4},{2,5},{3,6},{4,7},{5,0},{6,1},{7,2},{8,11},{9,12},{10,... | collective-permute-start | bytes 294920 | tf_op jit(solution)/shard_map/ppermute | solution.py:22
  12.0 14.6 %collective-permute-start.3 = (bf16[3,4,4096]{2,1,0:T(4,128)(2,1)S(1)}, bf16[3,4,4096]{2,1,0:T(4,128)(2,1)}, u32[]{:S(2)}, u32[]{:S(2)}) collective-permute-start(bf16[3,4,4096]{2,1,0:T(4,128)(2,1)S(1)} %get-tuple-element.105), channel_id=1, source_target_pairs={{0,4},{1,5},{2,6},{3,7},{4,0},{5,1},{6,2},{7,3},{8,12},{9,13},{10,... | collective-permute-start | bytes 294920 | tf_op jit(solution)/shard_map/ppermute | solution.py:22
  13.3 14.3 %collective-permute-start.4 = (bf16[3,4,4096]{2,1,0:T(4,128)(2,1)S(1)}, bf16[3,4,4096]{2,1,0:T(4,128)(2,1)S(1)}, u32[]{:S(2)}, u32[]{:S(2)}) collective-permute-start(bf16[3,4,4096]{2,1,0:T(4,128)(2,1)S(1)} %get-tuple-element.104), channel_id=1, source_target_pairs={{0,5},{1,6},{2,7},{3,0},{4,1},{5,2},{6,3},{7,4},{8,13},{9,14},{10,... | collective-permute-start | bytes 294920 | tf_op jit(solution)/shard_map/ppermute | solution.py:22
  16.3 27.0 %all-to-all-start = ((bf16[8,3,4,4096]{3,2,1,0:T(4,128)(2,1)}), bf16[8,3,4,4096]{3,2,1,0:T(4,128)(2,1)S(1)}, u32[]{:S(2)}, u32[]{:S(2)}) async-start(bf16[8,3,4,4096]{3,2,1,0:T(4,128)(2,1)} %copy.106), calls=%async_computation | async-start | bytes 1572864 | tf_op jit(solution)/shard_map/all_to_all | solution.py:114
  19.9 16.5 %collective-permute-start.5 = (bf16[3,4,4096]{2,1,0:T(4,128)(2,1)S(1)}, bf16[3,4,4096]{2,1,0:T(4,128)(2,1)S(1)}, u32[]{:S(2)}, u32[]{:S(2)}) collective-permute-start(bf16[3,4,4096]{2,1,0:T(4,128)(2,1)S(1)} %get-tuple-element.103), channel_id=1, source_target_pairs={{0,6},{1,7},{2,0},{3,1},{4,2},{5,3},{6,4},{7,5},{8,14},{9,15},{10,... | collective-permute-start | bytes 294920 | tf_op jit(solution)/shard_map/ppermute | solution.py:22
  24.7 12.1 %collective-permute-start.6 = (bf16[3,4,4096]{2,1,0:T(4,128)(2,1)S(1)}, bf16[3,4,4096]{2,1,0:T(4,128)(2,1)S(1)}, u32[]{:S(2)}, u32[]{:S(2)}) collective-permute-start(bf16[3,4,4096]{2,1,0:T(4,128)(2,1)S(1)} %get-tuple-element.102), channel_id=1, source_target_pairs={{0,7},{1,0},{2,1},{3,2},{4,3},{5,4},{6,5},{7,6},{8,15},{9,8},{10,9... | collective-permute-start | bytes 294920 | tf_op jit(solution)/shard_map/ppermute | solution.py:22
  50.9 36.5 %copy-start.43 = (bf16[1,16,8,2]{1,3,2,0:T(2,128)(2,1)S(1)}, bf16[1,16,8,2]{1,3,2,0:T(2,128)(2,1)}, u32[]{:S(2)}) copy-start(bf16[1,16,8,2]{1,3,2,0:T(2,128)(2,1)} %param.27) | copy-start | bytes 1540
  52.1 35.3 %copy-start.29 = (s32[16,8,2,8]{0,3,2,1:T(8,128)S(1)}, s32[16,8,2,8]{0,3,2,1:T(8,128)}, u32[]{:S(2)}) copy-start(s32[16,8,2,8]{0,3,2,1:T(8,128)} %copy-done.28) | copy-start | bytes 24580
  52.1 31.5 %all-to-all-start.1 = ((bf16[8,3,4,4096]{3,2,1,0:T(4,128)(2,1)}), bf16[8,3,4,4096]{3,2,1,0:T(4,128)(2,1)S(1)}, u32[]{:S(2)}, u32[]{:S(2)}) async-start(bf16[8,3,4,4096]{3,2,1,0:T(4,128)(2,1)} %reshape.354), calls=%async_computation.1 | async-start | bytes 1572864 | tf_op jit(solution)/shard_map/all_to_all | solution.py:118
  65.5 47.0 %copy-start.25 = (f32[1,96,512]{2,1,0:T(8,128)S(1)}, f32[1,96,512]{2,1,0:T(8,128)}, u32[]{:S(2)}) copy-start(f32[1,96,512]{2,1,0:T(8,128)} %copy-done.24) | copy-start | bytes 589828
  65.5 47.2 %copy-start.23 = (f32[1,96,512]{2,1,0:T(8,128)S(1)}, f32[1,96,512]{2,1,0:T(8,128)}, u32[]{:S(2)}) copy-start(f32[1,96,512]{2,1,0:T(8,128)} %multiply_bitcast_fusion) | copy-start | bytes 589828
  83.6 24.7 %all-to-all-start.3 = ((bf16[8,3,4,4096]{3,2,1,0:T(4,128)(2,1)}), bf16[8,3,4,4096]{3,2,1,0:T(4,128)(2,1)S(1)}, u32[]{:S(2)}, u32[]{:S(2)}) async-start(bf16[8,3,4,4096]{3,2,1,0:T(4,128)(2,1)} %copy.110), calls=%async_computation.3 | async-start | bytes 1572864 | tf_op jit(solution)/shard_map/all_to_all | solution.py:89
  87.6 25.0 %copy-start.42 = (bf16[16,8,8,3]{2,1,3,0:T(8,128)(2,1)}, bf16[16,8,8,3]{2,1,3,0:T(8,128)(2,1)S(1)}, u32[]{:S(2)}) copy-start(bf16[16,8,8,3]{2,1,3,0:T(8,128)(2,1)S(1)} %copy.104) | copy-start | bytes 18436
  88.5 24.1 %copy-start.30 = (bf16[4,8,4096]{2,1,0:T(8,128)(2,1)}, bf16[4,8,4096]{2,1,0:T(8,128)(2,1)S(1)}, u32[]{:S(2)}) copy-start(bf16[4,8,4096]{2,1,0:T(8,128)(2,1)S(1)} %fusion.19) | copy-start | bytes 786436
  88.5 10.9 %collective-permute-start.7 = (bf16[4,8,4096]{2,1,0:T(8,128)(2,1)S(1)}, bf16[4,8,4096]{2,1,0:T(8,128)(2,1)}, u32[]{:S(2)}, u32[]{:S(2)}) collective-permute-start(bf16[4,8,4096]{2,1,0:T(8,128)(2,1)S(1)} %fusion.19), channel_id=1, source_target_pairs={{8,0},{16,8},{24,16},{9,1},{17,9},{25,17},{10,2},{18,10},{26,18},{... | collective-permute-start | bytes 786440 | tf_op jit(solution)/shard_map/ppermute | solution.py:14
  108.3 4.2 copy-start.19
  108.3 25.2 %all-to-all-start.2 = ((bf16[8,3,4,4096]{3,2,1,0:T(4,128)(2,1)}), bf16[8,3,4,4096]{3,2,1,0:T(4,128)(2,1)}, u32[]{:S(2)}, u32[]{:S(2)}) async-start(bf16[8,3,4,4096]{3,2,1,0:T(4,128)(2,1)} %copy.109), calls=%async_computation.2 | async-start | bytes 1572864 | tf_op jit(solution)/shard_map/all_to_all | solution.py:114
  143.6 24.5 %all-to-all-start.4 = ((bf16[8,3,4,4096]{3,2,1,0:T(4,128)(2,1)}), bf16[8,3,4,4096]{3,2,1,0:T(4,128)(2,1)S(1)}, u32[]{:S(2)}, u32[]{:S(2)}) async-start(bf16[8,3,4,4096]{3,2,1,0:T(4,128)(2,1)} %reshape.359), calls=%async_computation.4 | async-start | bytes 1572864 | tf_op jit(solution)/shard_map/all_to_all | solution.py:118
  168.9 24.4 %all-to-all-start.6 = ((bf16[8,3,4,4096]{3,2,1,0:T(4,128)(2,1)}), bf16[8,3,4,4096]{3,2,1,0:T(4,128)(2,1)S(1)}, u32[]{:S(2)}, u32[]{:S(2)}) async-start(bf16[8,3,4,4096]{3,2,1,0:T(4,128)(2,1)} %copy.113), calls=%async_computation.6 | async-start | bytes 1572864 | tf_op jit(solution)/shard_map/all_to_all | solution.py:89
  175.3 11.1 %collective-permute-start.8 = (bf16[4,8,4096]{2,1,0:T(8,128)(2,1)}, bf16[4,8,4096]{2,1,0:T(8,128)(2,1)}, u32[]{:S(2)}, u32[]{:S(2)}) collective-permute-start(bf16[4,8,4096]{2,1,0:T(8,128)(2,1)} %add_convert_fusion.5), channel_id=1, source_target_pairs={{8,0},{16,8},{24,16},{9,1},{17,9},{25,17},{10,2},{18,10},{26,18},{... | collective-permute-start | bytes 786440 | tf_op jit(solution)/shard_map/ppermute | solution.py:14
  193.4 4.6 copy-start.20
  193.4 25.6 %all-to-all-start.5 = ((bf16[8,3,4,4096]{3,2,1,0:T(4,128)(2,1)}), bf16[8,3,4,4096]{3,2,1,0:T(4,128)(2,1)}, u32[]{:S(2)}, u32[]{:S(2)}) async-start(bf16[8,3,4,4096]{3,2,1,0:T(4,128)(2,1)} %copy.112), calls=%async_computation.5 | async-start | bytes 1572864 | tf_op jit(solution)/shard_map/all_to_all | solution.py:114
  229.1 24.5 %all-to-all-start.7 = ((bf16[8,3,4,4096]{3,2,1,0:T(4,128)(2,1)}), bf16[8,3,4,4096]{3,2,1,0:T(4,128)(2,1)S(1)}, u32[]{:S(2)}, u32[]{:S(2)}) async-start(bf16[8,3,4,4096]{3,2,1,0:T(4,128)(2,1)} %reshape.364), calls=%async_computation.7 | async-start | bytes 1572864 | tf_op jit(solution)/shard_map/all_to_all | solution.py:118
  254.4 24.4 %all-to-all-start.9 = ((bf16[8,3,4,4096]{3,2,1,0:T(4,128)(2,1)}), bf16[8,3,4,4096]{3,2,1,0:T(4,128)(2,1)S(1)}, u32[]{:S(2)}, u32[]{:S(2)}) async-start(bf16[8,3,4,4096]{3,2,1,0:T(4,128)(2,1)} %copy.116), calls=%async_computation.9 | async-start | bytes 1572864 | tf_op jit(solution)/shard_map/all_to_all | solution.py:89
  260.8 11.1 %collective-permute-start.9 = (bf16[4,8,4096]{2,1,0:T(8,128)(2,1)}, bf16[4,8,4096]{2,1,0:T(8,128)(2,1)}, u32[]{:S(2)}, u32[]{:S(2)}) collective-permute-start(bf16[4,8,4096]{2,1,0:T(8,128)(2,1)} %add_convert_fusion.4), channel_id=1, source_target_pairs={{8,0},{16,8},{24,16},{9,1},{17,9},{25,17},{10,2},{18,10},{26,18},{... | collective-permute-start | bytes 786440 | tf_op jit(solution)/shard_map/ppermute | solution.py:14
  278.8 4.4 copy-start.21
  278.8 25.4 %all-to-all-start.8 = ((bf16[8,3,4,4096]{3,2,1,0:T(4,128)(2,1)}), bf16[8,3,4,4096]{3,2,1,0:T(4,128)(2,1)}, u32[]{:S(2)}, u32[]{:S(2)}) async-start(bf16[8,3,4,4096]{3,2,1,0:T(4,128)(2,1)} %copy.115), calls=%async_computation.8 | async-start | bytes 1572864 | tf_op jit(solution)/shard_map/all_to_all | solution.py:114
  341.0 15.9 %copy-start.32 = (bf16[4,8,4096]{2,1,0:T(8,128)(2,1)}, bf16[4,8,4096]{2,1,0:T(8,128)(2,1)S(1)}, u32[]{:S(2)}) copy-start(bf16[4,8,4096]{2,1,0:T(8,128)(2,1)S(1)} %add_convert_fusion.3) | copy-start | bytes 786436
  341.0 9.8 %collective-permute-start.10 = (bf16[4,8,4096]{2,1,0:T(8,128)(2,1)S(1)}, bf16[4,8,4096]{2,1,0:T(8,128)(2,1)S(1)}, u32[]{:S(2)}, u32[]{:S(2)}) collective-permute-start(bf16[4,8,4096]{2,1,0:T(8,128)(2,1)S(1)} %add_convert_fusion.3), channel_id=1, source_target_pairs={{8,0},{16,8},{24,16},{9,1},{17,9},{25,17},{10,2},{18,10},{26,18},{... | collective-permute-start | bytes 786440 | tf_op jit(solution)/shard_map/ppermute | solution.py:14
  350.8 6.1 %copy-start.41 = (bf16[4,8,4096]{2,1,0:T(8,128)(2,1)}, bf16[4,8,4096]{2,1,0:T(8,128)(2,1)S(1)}, u32[]{:S(2)}) copy-start(bf16[4,8,4096]{2,1,0:T(8,128)(2,1)S(1)} %collective-permute-done.10) | copy-start | bytes 786436
  352.7 25.2 %all-to-all-start.11 = ((bf16[8,3,4,4096]{3,2,1,0:T(4,128)(2,1)}), bf16[8,3,4,4096]{3,2,1,0:T(4,128)(2,1)}, u32[]{:S(2)}, u32[]{:S(2)}) async-start(bf16[8,3,4,4096]{3,2,1,0:T(4,128)(2,1)} %copy.118), calls=%async_computation.11 | async-start | bytes 1572864 | tf_op jit(solution)/shard_map/all_to_all | solution.py:114
  414.9 16.5 %copy-start.34 = (bf16[4,8,4096]{2,1,0:T(8,128)(2,1)}, bf16[4,8,4096]{2,1,0:T(8,128)(2,1)S(1)}, u32[]{:S(2)}) copy-start(bf16[4,8,4096]{2,1,0:T(8,128)(2,1)S(1)} %add_convert_fusion.2) | copy-start | bytes 786436
  414.9 10.5 %collective-permute-start.11 = (bf16[4,8,4096]{2,1,0:T(8,128)(2,1)S(1)}, bf16[4,8,4096]{2,1,0:T(8,128)(2,1)S(1)}, u32[]{:S(2)}, u32[]{:S(2)}) collective-permute-start(bf16[4,8,4096]{2,1,0:T(8,128)(2,1)S(1)} %add_convert_fusion.2), channel_id=1, source_target_pairs={{8,0},{16,8},{24,16},{9,1},{17,9},{25,17},{10,2},{18,10},{26,18},{... | collective-permute-start | bytes 786440 | tf_op jit(solution)/shard_map/ppermute | solution.py:14
  425.3 6.1 %copy-start.40 = (bf16[4,8,4096]{2,1,0:T(8,128)(2,1)}, bf16[4,8,4096]{2,1,0:T(8,128)(2,1)S(1)}, u32[]{:S(2)}) copy-start(bf16[4,8,4096]{2,1,0:T(8,128)(2,1)S(1)} %collective-permute-done.11) | copy-start | bytes 786436
  427.2 25.2 %all-to-all-start.13 = ((bf16[8,3,4,4096]{3,2,1,0:T(4,128)(2,1)}), bf16[8,3,4,4096]{3,2,1,0:T(4,128)(2,1)}, u32[]{:S(2)}, u32[]{:S(2)}) async-start(bf16[8,3,4,4096]{3,2,1,0:T(4,128)(2,1)} %copy.120), calls=%async_computation.13 | async-start | bytes 1572864 | tf_op jit(solution)/shard_map/all_to_all | solution.py:114
  487.3 19.9 %copy-start.31 = (bf16[4,8,4096]{2,1,0:T(8,128)(2,1)S(1)}, bf16[4,8,4096]{2,1,0:T(8,128)(2,1)}, u32[]{:S(2)}) copy-start(bf16[4,8,4096]{2,1,0:T(8,128)(2,1)} %copy-done.30) | copy-start | bytes 786436
  489.2 20.3 %copy-start.36 = (bf16[4,8,4096]{2,1,0:T(8,128)(2,1)}, bf16[4,8,4096]{2,1,0:T(8,128)(2,1)S(1)}, u32[]{:S(2)}) copy-start(bf16[4,8,4096]{2,1,0:T(8,128)(2,1)S(1)} %add_convert_fusion.1) | copy-start | bytes 786436
  489.2 10.5 %collective-permute-start.12 = (bf16[4,8,4096]{2,1,0:T(8,128)(2,1)S(1)}, bf16[4,8,4096]{2,1,0:T(8,128)(2,1)S(1)}, u32[]{:S(2)}, u32[]{:S(2)}) collective-permute-start(bf16[4,8,4096]{2,1,0:T(8,128)(2,1)S(1)} %add_convert_fusion.1), channel_id=1, source_target_pairs={{8,0},{16,8},{24,16},{9,1},{17,9},{25,17},{10,2},{18,10},{26,18},{... | collective-permute-start | bytes 786440 | tf_op jit(solution)/shard_map/ppermute | solution.py:14
  499.7 9.9 %copy-start.38 = (bf16[4,8,4096]{2,1,0:T(8,128)(2,1)}, bf16[4,8,4096]{2,1,0:T(8,128)(2,1)S(1)}, u32[]{:S(2)}) copy-start(bf16[4,8,4096]{2,1,0:T(8,128)(2,1)S(1)} %collective-permute-done.12) | copy-start | bytes 786436
  501.5 25.2 %all-to-all-start.15 = ((bf16[8,3,4,4096]{3,2,1,0:T(4,128)(2,1)}), bf16[8,3,4,4096]{3,2,1,0:T(4,128)(2,1)}, u32[]{:S(2)}, u32[]{:S(2)}) async-start(bf16[8,3,4,4096]{3,2,1,0:T(4,128)(2,1)} %copy.122), calls=%async_computation.15 | async-start | bytes 1572864 | tf_op jit(solution)/shard_map/all_to_all | solution.py:114
  534.3 7.8 %copy-start.33 = (bf16[4,8,4096]{2,1,0:T(8,128)(2,1)S(1)}, bf16[4,8,4096]{2,1,0:T(8,128)(2,1)}, u32[]{:S(2)}) copy-start(bf16[4,8,4096]{2,1,0:T(8,128)(2,1)} %copy-done.32) | copy-start | bytes 786436
  534.3 8.5 %copy-start.35 = (bf16[4,8,4096]{2,1,0:T(8,128)(2,1)S(1)}, bf16[4,8,4096]{2,1,0:T(8,128)(2,1)}, u32[]{:S(2)}) copy-start(bf16[4,8,4096]{2,1,0:T(8,128)(2,1)} %copy-done.34) | copy-start | bytes 786436
  534.3 9.3 %copy-start.37 = (bf16[4,8,4096]{2,1,0:T(8,128)(2,1)S(1)}, bf16[4,8,4096]{2,1,0:T(8,128)(2,1)}, u32[]{:S(2)}) copy-start(bf16[4,8,4096]{2,1,0:T(8,128)(2,1)} %copy-done.36) | copy-start | bytes 786436
  535.7 25.6 %copy-start.39 = (bf16[4,8,4096]{2,1,0:T(8,128)(2,1)S(1)}, bf16[4,8,4096]{2,1,0:T(8,128)(2,1)}, u32[]{:S(2)}) copy-start(bf16[4,8,4096]{2,1,0:T(8,128)(2,1)} %copy-done.38) | copy-start | bytes 786436
  536.8 24.5 %all-to-all-start.16 = ((bf16[8,3,4,4096]{3,2,1,0:T(4,128)(2,1)}), bf16[8,3,4,4096]{3,2,1,0:T(4,128)(2,1)S(1)}, u32[]{:S(2)}, u32[]{:S(2)}) async-start(bf16[8,3,4,4096]{3,2,1,0:T(4,128)(2,1)} %reshape.375), calls=%async_computation.16 | async-start | bytes 1572864 | tf_op jit(solution)/shard_map/all_to_all | solution.py:118
  (23 other events, 65.4 us)
